TPU v7x, 256 devices: a whole 4x4x8 slice. The times are simulated.
256 devices in a mesh: hid: 32 (over z_hi, x, core), wid: 8 (over z_lo, y).
Axes of the slice: x: 4, y: 4, z: 8 (z_hi: 4, z_lo: 2; z = z_hi * 2 + z_lo), core: 2. Of those that a mesh axis runs over, the one named last changes fastest.
Arguments:
- inputs: bfloat16 [768, 8192], P('hid', 'wid'), may hold values from -6 to 6
- gate_weight: bfloat16 [8192, 28672], P('wid', 'hid'), may hold values from -0.0625 to 0.0625
- up_weight: bfloat16 [8192, 28672], P('wid', 'hid'), may hold values from -0.0625 to 0.0625
- down_weight: bfloat16 [28672, 8192], P('hid', 'wid'), may hold values from -0.03125 to 0.03125
- out_grad: bfloat16 [768, 8192], P('hid', 'wid'), may hold values from -0.43164062 to 0.43164062
Outputs:
- input_grad: bfloat16 [768, 8192], P('hid', 'wid')
- gate_grad: bfloat16 [8192, 28672], P('wid', 'hid')
- up_grad: bfloat16 [8192, 28672], P('wid', 'hid')
- down_grad: bfloat16 [28672, 8192], P('hid', 'wid')
All inputs are finite; a program needn't handle non-finite values.
Results may differ from a plain program's by a relative error of at most 0.02.
Values may be sent and summed in bfloat16 or wider, within the bound.
No kernel may reach another device: no remote copies, remote signals or barrier semaphores. Data moves between devices by JAX's collectives and lax.ppermute only.
A program may use at most 64 MiB of HBM per device.

v0:
```python
import jax
import jax.numpy as jnp
from jax import lax
from jax.sharding import PartitionSpec as P


def swiglu_terms(gate, up, hidden_grad):
    sigma = jax.nn.sigmoid(gate)
    hidden = (gate * sigma * up).astype(jnp.bfloat16)
    up_term = (hidden_grad * gate * sigma).astype(jnp.bfloat16)
    gate_term = (hidden_grad * up * sigma * (1.0 + gate * (1.0 - sigma))).astype(jnp.bfloat16)
    return (hidden, gate_term, up_term)


def per_device(inputs, gate_weight, up_weight, down_weight, out_grad):
    all_inputs, all_grads = (
        lax.all_gather(inputs, "hid", axis=0, tiled=True),
        lax.all_gather(out_grad, "hid", axis=0, tiled=True),
    )
    contract_last = (((1,), (1,)), ((), ()))
    gate_part = jnp.dot(all_inputs, gate_weight, preferred_element_type=jnp.float32)
    up_part = jnp.dot(all_inputs, up_weight, preferred_element_type=jnp.float32)
    grad_part = lax.dot_general(
        all_grads, down_weight, contract_last, preferred_element_type=jnp.float32
    )
    gate, up, hidden_grad = (
        lax.psum(gate_part.astype(jnp.bfloat16), "wid").astype(jnp.float32),
        lax.psum(up_part.astype(jnp.bfloat16), "wid").astype(jnp.float32),
        lax.psum(grad_part.astype(jnp.bfloat16), "wid").astype(jnp.float32),
    )
    hidden, gate_term, up_term = swiglu_terms(gate, up, hidden_grad)
    total = lax.dot_general(
        gate_term, gate_weight, contract_last, preferred_element_type=jnp.float32
    )
    input_grad = lax.psum_scatter(
        total
        + lax.dot_general(up_term, up_weight, contract_last, preferred_element_type=jnp.float32),
        "hid",
        scatter_dimension=0,
        tiled=True,
    ).astype(jnp.bfloat16)
    contract_first = (((0,), (0,)), ((), ()))
    gate_grad = lax.dot_general(
        all_inputs, gate_term, contract_first, preferred_element_type=jnp.float32
    ).astype(jnp.bfloat16)
    up_grad = lax.dot_general(
        all_inputs, up_term, contract_first, preferred_element_type=jnp.float32
    ).astype(jnp.bfloat16)
    down_grad = lax.dot_general(
        hidden, all_grads, contract_first, preferred_element_type=jnp.float32
    ).astype(jnp.bfloat16)
    return (input_grad, gate_grad, up_grad, down_grad)


def solution(mesh):
    placed = (P("hid", "wid"), P("wid", "hid"), P("wid", "hid"), P("hid", "wid"), P("hid", "wid"))
    return jax.shard_map(
        per_device,
        mesh=mesh,
        in_specs=placed,
        out_specs=(P("hid", "wid"), P("wid", "hid"), P("wid", "hid"), P("hid", "wid")),
        check_vma=False,
    )
```

profile of v0, /device:TPU:32, one launch (start us, length us, event | category | flops | bytes accessed | tf_op | source)
XLA Modules:
  0.0 342.9 jit_solution(14188217543889474345)
XLA Ops:
  7.2 0.0 all-gather.5.cloned.1.call-start
  7.2 0.7 all-gather.5.cloned.1.call-update
  7.9 0.0 all-gather.3.cloned.1.call-start
  8.0 0.7 all-gather.3.cloned.1.call-update
  8.7 0.0 all-reduce.3.cloned.1.call-start
  8.7 56.1 %all-gather.5.cloned.1.call-done = bf16[768,1024]{1,0:T(8,128)(2,1)} async-done(((bf16[24,1024]{1,0:T(8,128)(2,1)}), bf16[768,1024]{1,0:T(8,128)(2,1)}) %all-gather.5.cloned.1.call-update) | async-done | bytes 1572880 | tf_op jit(solution)/shard_map/all_gather | solution.py:17
  64.8 4.4 %convolution_convert_fusion.1 = bf16[768,896]{1,0:T(8,128)(2,1)} fusion(bf16[768,1024]{1,0:T(8,128)(2,1)} %all-gather.5.cloned.1.call-done, bf16[1024,896]{1,0:T(8,128)(2,1)S(1)} %copy-done), kind=kOutput, calls=%fused_computation.20 | convolution fusion | flops 1409974272 | bytes 4784128 | tf_op jit(solution)/shard_map/dot_general | solution.py:21
  69.2 2.9 convolution_convert_fusion.2
  72.1 45.4 %all-gather.3.cloned.1.call-done = bf16[768,1024]{1,0:T(8,128)(2,1)} async-done(((bf16[24,1024]{1,0:T(8,128)(2,1)}), bf16[768,1024]{1,0:T(8,128)(2,1)}) %all-gather.3.cloned.1.call-update) | async-done | bytes 1572880 | tf_op jit(solution)/shard_map/all_gather | solution.py:18
  117.5 4.9 %convolution_convert_fusion.3 = bf16[768,896]{1,0:T(8,128)(2,1)} fusion(bf16[768,1024]{1,0:T(8,128)(2,1)} %all-gather.3.cloned.1.call-done, bf16[896,1024]{1,0:T(8,128)(2,1)} %param.8), kind=kOutput, calls=%fused_computation.22 | convolution fusion | flops 1409974272 | bytes 4784128 | tf_op jit(solution)/shard_map/dot_general | solution.py:23
  122.4 0.2 reduce-scatter.2.cloned.1.call-start
  122.6 106.8 %all-reduce.3.cloned.1.call-done = (bf16[768,896]{1,0:T(8,128)(2,1)}, bf16[768,896]{1,0:T(8,128)(2,1)}, bf16[768,896]{1,0:T(8,128)(2,1)}) async-done(((bf16[768,896]{1,0:T(8,128)(2,1)}, bf16[768,896]{1,0:T(8,128)(2,1)}, bf16[768,896]{1,0:T(8,128)(2,1)}), (bf16[768,896]{1,0:T(8,128)(2,1)}, bf16[768,896]{1,0:T(8,128)(2,1)}, bf16[768,896]{1,0:T(8,128)(2,1)})) %all-reduce.3.cloned.1.call-update) | async-done | bytes 4128784 | tf_op jit(solution)/shard_map/psum | solution.py:28
  229.5 3.4 fusion.2
  232.9 1.1 copy-done.4
  234.0 1.8 fusion.15
  235.8 0.5 copy-done.6
  236.3 3.6 %convolution_add_fusion = f32[768,1024]{1,0:T(8,128)} fusion(f32[768,1024]{1,0:T(8,128)S(1)} %fusion.15, bf16[1024,896]{1,0:T(8,128)(2,1)S(1)} %copy-done.6, bf16[768,896]{1,0:T(8,128)(2,1)S(1)} %copy-done.2, bf16[768,896]{1,0:T(8,128)(2,1)S(1)} %copy-done.3), kind=kOutput, calls=%fused_computation.19 | convolution fusion | flops 1415577600 | bytes 10878976 | tf_op jit(solution)/shard_map/dot_general | solution.py:37
  239.9 4.7 %convert_bitcast_fusion.1 = bf16[1024,896]{0,1:T(8,128)(2,1)} fusion(bf16[768,896]{1,0:T(8,128)(2,1)} %copy-done.4, bf16[768,1024]{1,0:T(8,128)(2,1)} %all-gather.5.cloned.1.call-done), kind=kOutput, calls=%fused_computation.17 | convolution fusion | flops 1410203648 | bytes 4784128 | tf_op jit(solution)/shard_map/dot_general | solution.py:43
  244.6 3.8 %copy.9 = bf16[1024,896]{1,0:T(8,128)(2,1)} copy(bf16[1024,896]{0,1:T(8,128)(2,1)} %convert_bitcast_fusion.1) | data formatting | bytes 3670016
  248.4 4.8 %convert_bitcast_fusion = bf16[1024,896]{0,1:T(8,128)(2,1)} fusion(bf16[768,1024]{1,0:T(8,128)(2,1)} %all-gather.5.cloned.1.call-done, bf16[768,896]{1,0:T(8,128)(2,1)S(1)} %copy-done.2, bf16[768,896]{1,0:T(8,128)(2,1)} %get-tuple-element.9), kind=kOutput, calls=%fused_computation.16 | convolution fusion | flops 1415708672 | bytes 6160384 | tf_op jit(solution)/shard_map/dot_general | solution.py:46
  253.2 3.9 %copy.10 = bf16[1024,896]{1,0:T(8,128)(2,1)} copy(bf16[1024,896]{0,1:T(8,128)(2,1)} %convert_bitcast_fusion) | data formatting | bytes 3670016
  257.1 4.9 %convolution_convert_fusion = bf16[896,1024]{1,0:T(8,128)(2,1)} fusion(bf16[768,1024]{1,0:T(8,128)(2,1)} %all-gather.3.cloned.1.call-done, bf16[768,896]{1,0:T(8,128)(2,1)S(1)} %copy-done.1, bf16[768,896]{1,0:T(8,128)(2,1)} %get-tuple-element.10), kind=kOutput, calls=%fused_computation.18 | convolution fusion | flops 1415708672 | bytes 6160384 | tf_op jit(solution)/shard_map/dot_general | solution.py:49
  262.0 72.8 %reduce-scatter.2.cloned.1.call-done = f32[24,1024]{1,0:T(8,128)} async-done(((f32[768,1024]{1,0:T(8,128)}), f32[24,1024]{1,0:T(8,128)}) %reduce-scatter.2.cloned.1.call-update) | async-done | bytes 98320 | tf_op jit(solution)/shard_map/reduce_scatter | solution.py:35
  334.9 1.5 convert_element_type.53
  (16 shorter events, 0.1 us)
Async XLA Ops:
  7.2 57.6 %copy-start = (bf16[1024,896]{1,0:T(8,128)(2,1)S(1)}, bf16[1024,896]{1,0:T(8,128)(2,1)}, u32[]{:S(2)}) copy-start(bf16[1024,896]{1,0:T(8,128)(2,1)} %param.6) | copy-start | bytes 5505028
  7.2 57.6 %all-gather.5.cloned.1.call-start = ((), (), s32[]{:S(2)}) async-start(), calls=%async_computation.2 | async-start | bytes 1622016 | tf_op jit(solution)/shard_map/all_gather | solution.py:17
  7.9 109.6 %all-gather.3.cloned.1.call-start = ((), (), s32[]{:S(2)}) async-start(), calls=%async_computation.1 | async-start | bytes 1622016 | tf_op jit(solution)/shard_map/all_gather | solution.py:18
  8.7 220.8 %all-reduce.3.cloned.1.call-start = ((), (), s32[]{:S(2)}) async-start(), calls=%async_computation.4 | async-start | bytes 8257536 | tf_op jit(solution)/shard_map/psum | solution.py:28
  64.8 4.4 %copy-start.5 = (bf16[1024,896]{1,0:T(8,128)(2,1)S(1)}, bf16[1024,896]{1,0:T(8,128)(2,1)}, u32[]{:S(2)}) copy-start(bf16[1024,896]{1,0:T(8,128)(2,1)} %param.7) | copy-start | bytes 5505028
  64.8 4.4 %copy-start.7 = (bf16[768,1024]{1,0:T(8,128)(2,1)S(1)}, bf16[768,1024]{1,0:T(8,128)(2,1)}, u32[]{:S(2)}) copy-start(bf16[768,1024]{1,0:T(8,128)(2,1)} %all-gather.5.cloned.1.call-done) | copy-start | bytes 4718596
  122.4 212.4 %reduce-scatter.2.cloned.1.call-start = ((), (), s32[]{:S(2)}) async-start(), calls=%async_computation.3 | async-start | bytes 3244032 | tf_op jit(solution)/shard_map/reduce_scatter | solution.py:35
  232.9 1.1 copy-start.4
  234.0 1.8 copy-start.2
  234.0 1.8 copy-start.3
  234.0 2.3 copy-start.6
  253.2 3.9 %copy-start.1 = (bf16[768,896]{1,0:T(8,128)(2,1)S(1)}, bf16[768,896]{1,0:T(8,128)(2,1)}, u32[]{:S(2)}) copy-start(bf16[768,896]{1,0:T(8,128)(2,1)} %get-tuple-element.8) | copy-start | bytes 4128772
Sparse Core Ops, SparseCore 0:
  10.5 54.1 all-gather.4
  67.3 50.1 all-gather.2
  122.5 106.8 all-reduce.2
  240.0 94.8 reduce-scatter.1
where the time goes:
time: 345 us; the launch traced here: 343 us
  waiting for transfers between devices  283 us (82%)
  matrix products  31.9 us (9%)
  between operations  13.8 us (4%)
  local copies, waits for them, and re-layouts  9.31 us (3%)
  other arithmetic  4.92 us (1%)
    psum x1, waiting for transfers between devices, per_device(): lax.psum(up_part.astype(jnp.bfloat16), 'wid').astype(jnp.float32)  107 us
    reduce_scatter x1, waiting for transfers between devices, per_device(): lax.psum_scatter(total + lax.dot_general(up_term, up_weight, contract_las...  72.8 us
    all_gather x1, waiting for transfers between devices, per_device(): lax.all_gather(inputs, 'hid', axis=0, tiled=True)  56.1 us
    all_gather x1, waiting for transfers between devices, per_device(): lax.all_gather(out_grad, 'hid', axis=0, tiled=True)  45.4 us
    unnamed x18, local copies, waits for them, and re-layouts  9.31 us
  transfers between devices with their start and end apart: 4, of which 4 were waited for; matrix products, arithmetic and copies ran while one was open for 9% of the time, Pallas kernels for 0%

commit v1 on v0

v1 whole, which is shorter than its diff:
```python
import jax
import jax.numpy as jnp
from jax import lax
from jax.sharding import PartitionSpec as P


def swiglu_terms(gate, up, hidden_grad):
    sigma = jax.nn.sigmoid(gate)
    hidden = (gate * sigma * up).astype(jnp.bfloat16)
    up_term = (hidden_grad * gate * sigma).astype(jnp.bfloat16)
    gate_term = (hidden_grad * up * sigma * (1.0 + gate * (1.0 - sigma))).astype(jnp.bfloat16)
    return (hidden, gate_term, up_term)


def make_per_device(n_hid, n_wid):
    def per_device(inputs, gate_weight, up_weight, down_weight, out_grad):
        dw = inputs.shape[1]
        ff = gate_weight.shape[1]
        both = lax.all_gather(jnp.concatenate([inputs, out_grad], 1), "hid", axis=0, tiled=True)
        all_inputs, all_grads = both[:, :dw], both[:, dw:]
        tokens = all_inputs.shape[0]
        contract_last = (((1,), (1,)), ((), ()))
        gate_part = jnp.dot(all_inputs, gate_weight, preferred_element_type=jnp.float32)
        up_part = jnp.dot(all_inputs, up_weight, preferred_element_type=jnp.float32)
        grad_part = lax.dot_general(
            all_grads, down_weight, contract_last, preferred_element_type=jnp.float32
        )
        parts = jnp.concatenate([gate_part, up_part, grad_part], 1).astype(jnp.bfloat16)
        parts = lax.all_to_all(parts.reshape(n_wid, tokens // n_wid, 3 * ff), "wid", 0, 0, tiled=False)
        sums = jnp.sum(parts.astype(jnp.float32), 0)
        gate, up, hidden_grad = sums[:, :ff], sums[:, ff:2 * ff], sums[:, 2 * ff:]
        terms = jnp.concatenate(swiglu_terms(gate, up, hidden_grad), 1)
        terms = jnp.broadcast_to(terms[None], (n_wid,) + terms.shape)
        terms = lax.all_to_all(terms, "wid", 0, 0, tiled=False).reshape(tokens, 3 * ff)
        hidden, gate_term, up_term = terms[:, :ff], terms[:, ff:2 * ff], terms[:, 2 * ff:]
        total = lax.dot_general(
            gate_term, gate_weight, contract_last, preferred_element_type=jnp.float32
        ) + lax.dot_general(up_term, up_weight, contract_last, preferred_element_type=jnp.float32)
        total = lax.all_to_all(total.reshape(n_hid, tokens // n_hid, dw), "hid", 0, 0, tiled=False)
        input_grad = jnp.sum(total, 0).astype(jnp.bfloat16)
        contract_first = (((0,), (0,)), ((), ()))
        gate_grad = lax.dot_general(
            all_inputs, gate_term, contract_first, preferred_element_type=jnp.float32
        ).astype(jnp.bfloat16)
        up_grad = lax.dot_general(
            all_inputs, up_term, contract_first, preferred_element_type=jnp.float32
        ).astype(jnp.bfloat16)
        down_grad = lax.dot_general(
            hidden, all_grads, contract_first, preferred_element_type=jnp.float32
        ).astype(jnp.bfloat16)
        return (input_grad, gate_grad, up_grad, down_grad)

    return per_device


def solution(mesh):
    placed = (P("hid", "wid"), P("wid", "hid"), P("wid", "hid"), P("hid", "wid"), P("hid", "wid"))
    return jax.shard_map(
        make_per_device(mesh.shape["hid"], mesh.shape["wid"]),
        mesh=mesh,
        in_specs=placed,
        out_specs=(P("hid", "wid"), P("wid", "hid"), P("wid", "hid"), P("hid", "wid")),
        check_vma=False,
    )
```

time: 345 us -> 283 us (0.82)
  the two profiles are of different devices: /device:TPU:32 before, /device:TPU:1 now
where the time goes in v1:
time: 283 us; the launch traced here: 282 us
  waiting for transfers between devices  127 us (45%)
  blocking collectives  103 us (36%)
  matrix products  23.9 us (8%)
  between operations  14.2 us (5%)
  starting transfers between devices  8.26 us (3%)
  other arithmetic  5.42 us (2%)
    all_to_all x1, waiting for transfers between devices, per_device(): lax.all_to_all(total.reshape(n_hid, tokens // n_hid, dw), 'hid', 0, 0, ti...  63.3 us
    all_gather x1, waiting for transfers between devices, per_device(): lax.all_gather(jnp.concatenate([inputs, out_grad], 1), 'hid', axis=0, til...  63.3 us
    all_to_all x1, blocking collectives, per_device(): lax.all_to_all(parts.reshape(n_wid, tokens // n_wid, 3 * ff), 'wid', 0, 0...  52.1 us
    all_to_all x1, blocking collectives, per_device(): lax.all_to_all(terms, 'wid', 0, 0, tiled=False).reshape(tokens, 3 * ff)  50.5 us
    all_to_all x1, starting transfers between devices, per_device(): lax.all_to_all(total.reshape(n_hid, tokens // n_hid, dw), 'hid', 0, 0, ti...  8.22 us
  transfers between devices with their start and end apart: 2, of which 2 were waited for; matrix products, arithmetic and copies ran while one was open for 4% of the time, Pallas kernels for 0%

profile of v1, /device:TPU:1, one launch (start us, length us, event | category | flops | bytes accessed | tf_op | source)
XLA Modules:
  0.0 282.4 jit_solution(664438621970241414)
XLA Ops:
  7.2 0.0 copy-start
  7.2 0.0 all-gather.2.cloned.1.call-start
  7.2 1.6 pad_maximum_fusion.2
  8.8 0.0 all-gather.2.cloned.1.call-update
  8.8 63.3 %all-gather.2.cloned.1.call-done = bf16[768,2048]{1,0:T(8,128)(2,1)} async-done(((bf16[24,2048]{1,0:T(8,128)(2,1)}), bf16[768,2048]{1,0:T(8,128)(2,1)}) %all-gather.2.cloned.1.call-update) | async-done | bytes 3145744 | tf_op jit(solution)/shard_map/all_gather | solution.py:19
  72.1 3.9 %convolution_convert_fusion.4 = bf16[768,896]{1,0:T(8,128)(2,1)S(1)} fusion(bf16[1024,896]{1,0:T(8,128)(2,1)} %param.7, bf16[768,2048]{1,0:T(8,128)(2,1)} %all-gather.2.cloned.1.call-done), kind=kOutput, calls=%fused_computation.7 | convolution fusion | flops 1409974272 | bytes 4784128 | tf_op jit(solution)/shard_map/dot_general | solution.py:24
  76.1 1.9 convolution_convert_fusion.3
  77.9 1.8 convolution_convert_fusion.5
  79.7 0.4 pad_maximum_fusion
  80.1 52.1 %all_to_all.15 = bf16[8,96,2688]{2,1,0:T(8,128)(2,1)S(1)} all-to-all(bf16[8,96,2688]{2,1,0:T(8,128)(2,1)S(1)} %pad_maximum_fusion), channel_id=1, replica_groups=mesh['hid'=32,'wid'=8] {'wid'}, dimensions={0} | all-to-all | bytes 8257536 | tf_op jit(solution)/shard_map/all_to_all | solution.py:29
  132.2 0.5 convert_reduce_fusion
  132.8 0.2 multiply_convert_fusion.2
  133.0 0.3 broadcast_in_dim.2
  133.3 50.5 %all_to_all.16 = bf16[8,96,2688]{2,1,0:T(8,128)(2,1)S(1)} all-to-all(bf16[8,96,2688]{2,1,0:T(8,128)(2,1)S(1)} %broadcast_in_dim.2), channel_id=1, replica_groups=mesh['hid'=32,'wid'=8] {'wid'}, dimensions={0} | all-to-all | bytes 8257536 | tf_op jit(solution)/shard_map/all_to_all | solution.py:34
  183.9 1.8 fusion.6
  185.7 0.2 copy-done.1
  185.9 0.8 copy-done.6
  186.7 3.6 %convolution_add_fusion = f32[768,1024]{1,0:T(8,128)} fusion(f32[768,1024]{1,0:T(8,128)S(1)} %fusion.6, bf16[1024,896]{1,0:T(8,128)(2,1)S(1)} %copy-done.6, bf16[768,2688]{1,0:T(8,128)(2,1)S(1)} %bitcast.11), kind=kOutput, calls=%fused_computation.5 | convolution fusion | flops 1410072576 | bytes 9502720 | tf_op jit(solution)/shard_map/dot_general | solution.py:38
  190.3 8.2 %all-to-all-start.2 = ((f32[32,24,1024]{2,1,0:T(8,128)}), f32[32,24,1024]{2,1,0:T(8,128)}, u32[]{:S(2)}, u32[]{:S(2)}) async-start(f32[32,24,1024]{2,1,0:T(8,128)} %bitcast.15), calls=%async_computation.2 | async-start | bytes 6291456 | tf_op jit(solution)/shard_map/all_to_all | solution.py:39
  198.6 5.0 %convolution_convert_fusion.2 = bf16[1024,896]{1,0:T(8,128)(2,1)} fusion(bf16[768,2688]{1,0:T(8,128)(2,1)} %bitcast.12, bf16[768,2048]{1,0:T(8,128)(2,1)} %all-gather.2.cloned.1.call-done), kind=kOutput, calls=%fused_computation.4 | convolution fusion | flops 1410203648 | bytes 4784128 | tf_op jit(solution)/shard_map/dot_general | solution.py:42
  203.6 3.1 %convolution_convert_fusion.1 = bf16[1024,896]{1,0:T(8,128)(2,1)} fusion(bf16[768,2688]{1,0:T(8,128)(2,1)S(1)} %bitcast.13, bf16[768,2048]{1,0:T(8,128)(2,1)S(1)} %copy-done.4), kind=kOutput, calls=%fused_computation.3 | convolution fusion | flops 1410203648 | bytes 4784128 | tf_op jit(solution)/shard_map/dot_general | solution.py:45
  206.7 2.9 %convolution_convert_fusion = bf16[896,1024]{1,0:T(8,128)(2,1)} fusion(bf16[768,2048]{1,0:T(8,128)(2,1)S(1)} %copy-done.4, bf16[768,2688]{1,0:T(8,128)(2,1)S(1)} %bitcast.14), kind=kOutput, calls=%fused_computation.2 | convolution fusion | flops 1410203648 | bytes 4784128 | tf_op jit(solution)/shard_map/dot_general | solution.py:48
  209.5 63.3 %all-to-all-done.2 = f32[32,24,1024]{2,1,0:T(8,128)} async-done(((f32[32,24,1024]{2,1,0:T(8,128)}), f32[32,24,1024]{2,1,0:T(8,128)}, u32[]{:S(2)}, u32[]{:S(2)}) %all-to-all-start.2) | async-done | bytes 3145760 | tf_op jit(solution)/shard_map/all_to_all | solution.py:39
  272.9 2.7 reduce_sum.19
  (12 shorter events, 0.1 us)
Async XLA Ops:
  7.2 70.8 %copy-start = (bf16[1024,896]{1,0:T(8,128)(2,1)S(1)}, bf16[1024,896]{1,0:T(8,128)(2,1)}, u32[]{:S(2)}) copy-start(bf16[1024,896]{1,0:T(8,128)(2,1)} %param.6) | copy-start | bytes 5505028
  7.2 64.9 %all-gather.2.cloned.1.call-start = ((), (), s32[]{:S(2)}) async-start(), calls=%async_computation.3 | async-start | bytes 3244032 | tf_op jit(solution)/shard_map/all_gather | solution.py:19
  72.1 3.9 %copy-start.3 = (bf16[768,2048]{1,0:T(8,128)(2,1)S(1)}, bf16[768,2048]{1,0:T(8,128)(2,1)}, u32[]{:S(2)}) copy-start(bf16[768,2048]{1,0:T(8,128)(2,1)} %all-gather.2.cloned.1.call-done) | copy-start | bytes 9437188
  72.1 3.9 %copy-start.5 = (bf16[896,1024]{1,0:T(8,128)(2,1)S(1)}, bf16[896,1024]{1,0:T(8,128)(2,1)}, u32[]{:S(2)}) copy-start(bf16[896,1024]{1,0:T(8,128)(2,1)} %param.8) | copy-start | bytes 5505028
  183.9 2.0 copy-start.1
  183.9 2.9 %copy-start.6 = (bf16[1024,896]{1,0:T(8,128)(2,1)S(1)}, bf16[1024,896]{1,0:T(8,128)(2,1)}, u32[]{:S(2)}) copy-start(bf16[1024,896]{1,0:T(8,128)(2,1)} %param.7) | copy-start | bytes 5505028
  190.3 82.6 %all-to-all-start.2 = ((f32[32,24,1024]{2,1,0:T(8,128)}), f32[32,24,1024]{2,1,0:T(8,128)}, u32[]{:S(2)}, u32[]{:S(2)}) async-start(f32[32,24,1024]{2,1,0:T(8,128)} %bitcast.15), calls=%async_computation.2 | async-start | bytes 6291456 | tf_op jit(solution)/shard_map/all_to_all | solution.py:39
  198.5 5.1 %copy-start.2 = (bf16[8,96,2688]{2,1,0:T(8,128)(2,1)S(1)}, bf16[8,96,2688]{2,1,0:T(8,128)(2,1)}, u32[]{:S(2)}) copy-start(bf16[8,96,2688]{2,1,0:T(8,128)(2,1)} %copy-done.1) | copy-start | bytes 12386308
  198.5 5.0 %copy-start.4 = (bf16[768,2048]{1,0:T(8,128)(2,1)S(1)}, bf16[768,2048]{1,0:T(8,128)(2,1)}, u32[]{:S(2)}) copy-start(bf16[768,2048]{1,0:T(8,128)(2,1)} %all-gather.2.cloned.1.call-done) | copy-start | bytes 9437188
Sparse Core Ops, SparseCore 0:
  11.1 60.9 all-gather.1

commit v2 on v1

--- a/solution.py
+++ b/solution.py
@@ -1,7 +1,7 @@
 import jax
 import jax.numpy as jnp
 from jax import lax
-from jax.sharding import PartitionSpec as P
+from jax.sharding import Mesh, PartitionSpec as P
 
 
 def swiglu_terms(gate, up, hidden_grad):
@@ -16,7 +16,7 @@
     def per_device(inputs, gate_weight, up_weight, down_weight, out_grad):
         dw = inputs.shape[1]
         ff = gate_weight.shape[1]
-        both = lax.all_gather(jnp.concatenate([inputs, out_grad], 1), "hid", axis=0, tiled=True)
+        both = lax.all_gather(jnp.concatenate([inputs, out_grad], 1), ("chip", "core"), axis=0, tiled=True)
         all_inputs, all_grads = both[:, :dw], both[:, dw:]
         tokens = all_inputs.shape[0]
         contract_last = (((1,), (1,)), ((), ()))
@@ -36,7 +36,9 @@
         total = lax.dot_general(
             gate_term, gate_weight, contract_last, preferred_element_type=jnp.float32
         ) + lax.dot_general(up_term, up_weight, contract_last, preferred_element_type=jnp.float32)
-        total = lax.all_to_all(total.reshape(n_hid, tokens // n_hid, dw), "hid", 0, 0, tiled=False)
+        total = total.reshape(n_hid // 2, 2, tokens // n_hid, dw)
+        total = jnp.sum(lax.all_to_all(total, "core", 1, 1, tiled=False), 1)
+        total = lax.all_to_all(total, "chip", 0, 0, tiled=False)
         input_grad = jnp.sum(total, 0).astype(jnp.bfloat16)
         contract_first = (((0,), (0,)), ((), ()))
         gate_grad = lax.dot_general(
@@ -54,11 +56,14 @@
 
 
 def solution(mesh):
-    placed = (P("hid", "wid"), P("wid", "hid"), P("wid", "hid"), P("hid", "wid"), P("hid", "wid"))
+    n_hid, n_wid = mesh.shape["hid"], mesh.shape["wid"]
+    split = Mesh(mesh.devices.reshape(n_hid // 2, 2, n_wid), ("chip", "core", "wid"))
+    hid = ("chip", "core")
+    placed = (P(hid, "wid"), P("wid", hid), P("wid", hid), P(hid, "wid"), P(hid, "wid"))
     return jax.shard_map(
-        make_per_device(mesh.shape["hid"], mesh.shape["wid"]),
-        mesh=mesh,
+        make_per_device(n_hid, n_wid),
+        mesh=split,
         in_specs=placed,
-        out_specs=(P("hid", "wid"), P("wid", "hid"), P("wid", "hid"), P("hid", "wid")),
+        out_specs=(P(hid, "wid"), P("wid", hid), P("wid", hid), P(hid, "wid")),
         check_vma=False,
     )

time: 283 us -> 256 us (0.905)
  waiting for transfers between devices: 127 us -> 92.8 us
  blocking collectives: 103 us -> 112 us
  starting transfers between devices: 8.26 us -> 5.32 us
    all_to_all x1, waiting for transfers between devices: 63.3 us -> 29.5 us  [per_device(): total = lax.all_to_all(total, 'chip', 0, 0, tiled=False)]
    all_to_all x0 -> x1, blocking collectives: none -> 9.49 us  [per_device(): total = jnp.sum(lax.all_to_all(total, 'core', 1, 1, tiled=False), 1)]
    reduce_sum x0 -> x1, other arithmetic: none -> 3.47 us  [per_device(): total = jnp.sum(lax.all_to_all(total, 'core', 1, 1, tiled=False), 1)]
    all_to_all x1, starting transfers between devices: 8.22 us -> 5.28 us  [per_device(): total = lax.all_to_all(total, 'chip', 0, 0, tiled=False)]
where the time goes in v2:
time: 256 us; the launch traced here: 255 us
  blocking collectives  112 us (44%)
  waiting for transfers between devices  92.8 us (36%)
  matrix products  22.2 us (9%)
  between operations  14.2 us (6%)
  other arithmetic  6.91 us (3%)
  starting transfers between devices  5.32 us (2%)
    all_gather x1, waiting for transfers between devices, per_device(): lax.all_gather(jnp.concatenate([inputs, out_grad], 1), ('chip', 'core'),...  63.3 us
    all_to_all x1, blocking collectives, per_device(): lax.all_to_all(parts.reshape(n_wid, tokens // n_wid, 3 * ff), 'wid', 0, 0...  52.1 us
    all_to_all x1, blocking collectives, per_device(): lax.all_to_all(terms, 'wid', 0, 0, tiled=False).reshape(tokens, 3 * ff)  50.5 us
    all_to_all x1, waiting for transfers between devices, per_device(): total = lax.all_to_all(total, 'chip', 0, 0, tiled=False)  29.5 us
    all_to_all x1, blocking collectives, per_device(): total = jnp.sum(lax.all_to_all(total, 'core', 1, 1, tiled=False), 1)  9.49 us
    all_to_all x1, starting transfers between devices, per_device(): total = lax.all_to_all(total, 'chip', 0, 0, tiled=False)  5.28 us
  transfers between devices with their start and end apart: 2, of which 2 were waited for; matrix products, arithmetic and copies ran while one was open for 4% of the time, Pallas kernels for 0%

profile of v2, /device:TPU:1, one launch (start us, length us, event | category | flops | bytes accessed | tf_op | source)
XLA Modules:
  0.0 255.3 jit_solution(7301803369280233295)
XLA Ops:
  7.2 1.6 pad_maximum_fusion.2
  8.8 63.3 %all-gather.2.cloned.1.call-done = bf16[768,2048]{1,0:T(8,128)(2,1)} async-done(((bf16[24,2048]{1,0:T(8,128)(2,1)}), bf16[768,2048]{1,0:T(8,128)(2,1)}) %all-gather.2.cloned.1.call-update) | async-done | bytes 3145744 | tf_op jit(solution)/shard_map/all_gather | solution.py:19
  72.1 3.9 %convolution_convert_fusion.4 = bf16[768,896]{1,0:T(8,128)(2,1)S(1)} fusion(bf16[1024,896]{1,0:T(8,128)(2,1)} %param.7, bf16[768,2048]{1,0:T(8,128)(2,1)} %all-gather.2.cloned.1.call-done), kind=kOutput, calls=%fused_computation.7 | convolution fusion | flops 1409974272 | bytes 4784128 | tf_op jit(solution)/shard_map/dot_general | solution.py:24
  76.1 1.9 convolution_convert_fusion.3
  77.9 1.8 convolution_convert_fusion.5
  79.7 0.4 pad_maximum_fusion
  80.1 52.1 %all_to_all.20 = bf16[8,96,2688]{2,1,0:T(8,128)(2,1)S(1)} all-to-all(bf16[8,96,2688]{2,1,0:T(8,128)(2,1)S(1)} %pad_maximum_fusion), channel_id=1, replica_groups=mesh['chip'=16,'core'=2,'wid'=8] {'wid'}, dimensions={0} | all-to-all | bytes 8257536 | tf_op jit(solution)/shard_map/all_to_all | solution.py:29
  132.2 0.5 convert_reduce_fusion
  132.8 0.2 multiply_convert_fusion.2
  133.0 0.3 broadcast_in_dim.2
  133.3 50.5 %all_to_all.21 = bf16[8,96,2688]{2,1,0:T(8,128)(2,1)S(1)} all-to-all(bf16[8,96,2688]{2,1,0:T(8,128)(2,1)S(1)} %broadcast_in_dim.2), channel_id=1, replica_groups=mesh['chip'=16,'core'=2,'wid'=8] {'wid'}, dimensions={0} | all-to-all | bytes 8257536 | tf_op jit(solution)/shard_map/all_to_all | solution.py:34
  183.9 1.8 fusion.6
  185.7 0.2 copy-done.1
  185.9 0.8 copy-done.6
  186.7 1.8 convolution_add_fusion
  188.6 0.4 copy.10
  188.9 9.5 %all_to_all.22 = f32[16,2,24,1024]{3,2,0,1:T(8,128)} all-to-all(f32[16,2,24,1024]{3,2,0,1:T(8,128)S(1)} %copy.10), channel_id=1, replica_groups=mesh['chip'=16,'core'=2,'wid'=8] {'core'}, dimensions={1} | all-to-all | bytes 6291456 | tf_op jit(solution)/shard_map/all_to_all | solution.py:40
  198.4 3.5 %reduce_sum.28 = f32[16,24,1024]{2,1,0:T(8,128)} reduce(f32[16,2,24,1024]{3,2,0,1:T(8,128)} %all_to_all.22, f32[]{:T(128)} %constant.0.clone.1), dimensions={1}, to_apply=%region_1.0 | reduce | flops 393216 | bytes 4718596 | tf_op jit(solution)/shard_map/reduce_sum | solution.py:40
  201.9 5.3 %all-to-all-start.3 = ((f32[16,24,1024]{2,1,0:T(8,128)}), f32[16,24,1024]{2,1,0:T(8,128)S(1)}, u32[]{:S(2)}, u32[]{:S(2)}) async-start(f32[16,24,1024]{2,1,0:T(8,128)} %reduce_sum.28), calls=%async_computation.3 | async-start | bytes 3145728 | tf_op jit(solution)/shard_map/all_to_all | solution.py:41
  207.2 5.0 %convolution_convert_fusion.2 = bf16[1024,896]{1,0:T(8,128)(2,1)} fusion(bf16[768,2688]{1,0:T(8,128)(2,1)} %bitcast.12, bf16[768,2048]{1,0:T(8,128)(2,1)} %all-gather.2.cloned.1.call-done), kind=kOutput, calls=%fused_computation.4 | convolution fusion | flops 1410203648 | bytes 4784128 | tf_op jit(solution)/shard_map/dot_general | solution.py:44
  212.3 3.1 %convolution_convert_fusion.1 = bf16[1024,896]{1,0:T(8,128)(2,1)} fusion(bf16[768,2688]{1,0:T(8,128)(2,1)S(1)} %bitcast.13, bf16[768,2048]{1,0:T(8,128)(2,1)S(1)} %copy-done.4), kind=kOutput, calls=%fused_computation.3 | convolution fusion | flops 1410203648 | bytes 4784128 | tf_op jit(solution)/shard_map/dot_general | solution.py:47
  215.3 2.9 %convolution_convert_fusion = bf16[896,1024]{1,0:T(8,128)(2,1)} fusion(bf16[768,2048]{1,0:T(8,128)(2,1)S(1)} %copy-done.4, bf16[768,2688]{1,0:T(8,128)(2,1)S(1)} %bitcast.14), kind=kOutput, calls=%fused_computation.2 | convolution fusion | flops 1410203648 | bytes 4784128 | tf_op jit(solution)/shard_map/dot_general | solution.py:50
  218.2 29.5 %all-to-all-done.3 = f32[16,24,1024]{2,1,0:T(8,128)S(1)} async-done(((f32[16,24,1024]{2,1,0:T(8,128)}), f32[16,24,1024]{2,1,0:T(8,128)S(1)}, u32[]{:S(2)}, u32[]{:S(2)}) %all-to-all-start.3) | async-done | bytes 1572896 | tf_op jit(solution)/shard_map/all_to_all | solution.py:41
  247.7 0.7 reduce_sum.29
  (15 shorter events, 0.1 us)
Async XLA Ops:
  7.2 70.8 %copy-start = (bf16[1024,896]{1,0:T(8,128)(2,1)S(1)}, bf16[1024,896]{1,0:T(8,128)(2,1)}, u32[]{:S(2)}) copy-start(bf16[1024,896]{1,0:T(8,128)(2,1)} %param.6) | copy-start | bytes 5505028
  7.2 64.9 %all-gather.2.cloned.1.call-start = ((), (), s32[]{:S(2)}) async-start(), calls=%async_computation.4 | async-start | bytes 3244032 | tf_op jit(solution)/shard_map/all_gather | solution.py:19
  72.1 3.9 %copy-start.3 = (bf16[768,2048]{1,0:T(8,128)(2,1)S(1)}, bf16[768,2048]{1,0:T(8,128)(2,1)}, u32[]{:S(2)}) copy-start(bf16[768,2048]{1,0:T(8,128)(2,1)} %all-gather.2.cloned.1.call-done) | copy-start | bytes 9437188
  72.1 3.9 %copy-start.5 = (bf16[896,1024]{1,0:T(8,128)(2,1)S(1)}, bf16[896,1024]{1,0:T(8,128)(2,1)}, u32[]{:S(2)}) copy-start(bf16[896,1024]{1,0:T(8,128)(2,1)} %param.8) | copy-start | bytes 5505028
  183.9 2.0 copy-start.1
  183.9 2.9 %copy-start.6 = (bf16[1024,896]{1,0:T(8,128)(2,1)S(1)}, bf16[1024,896]{1,0:T(8,128)(2,1)}, u32[]{:S(2)}) copy-start(bf16[1024,896]{1,0:T(8,128)(2,1)} %param.7) | copy-start | bytes 5505028
  201.9 45.8 %all-to-all-start.3 = ((f32[16,24,1024]{2,1,0:T(8,128)}), f32[16,24,1024]{2,1,0:T(8,128)S(1)}, u32[]{:S(2)}, u32[]{:S(2)}) async-start(f32[16,24,1024]{2,1,0:T(8,128)} %reduce_sum.28), calls=%async_computation.3 | async-start | bytes 3145728 | tf_op jit(solution)/shard_map/all_to_all | solution.py:41
  207.2 5.1 %copy-start.2 = (bf16[8,96,2688]{2,1,0:T(8,128)(2,1)S(1)}, bf16[8,96,2688]{2,1,0:T(8,128)(2,1)}, u32[]{:S(2)}) copy-start(bf16[8,96,2688]{2,1,0:T(8,128)(2,1)} %copy-done.1) | copy-start | bytes 12386308
  207.2 5.0 %copy-start.4 = (bf16[768,2048]{1,0:T(8,128)(2,1)S(1)}, bf16[768,2048]{1,0:T(8,128)(2,1)}, u32[]{:S(2)}) copy-start(bf16[768,2048]{1,0:T(8,128)(2,1)} %all-gather.2.cloned.1.call-done) | copy-start | bytes 9437188
Sparse Core Ops, SparseCore 0:
  11.1 60.9 all-gather.1

commit v3 on v2

--- a/solution.py
+++ b/solution.py
@@ -38,8 +38,8 @@
         ) + lax.dot_general(up_term, up_weight, contract_last, preferred_element_type=jnp.float32)
         total = total.reshape(n_hid // 2, 2, tokens // n_hid, dw)
         total = jnp.sum(lax.all_to_all(total, "core", 1, 1, tiled=False), 1)
-        total = lax.all_to_all(total, "chip", 0, 0, tiled=False)
-        input_grad = jnp.sum(total, 0).astype(jnp.bfloat16)
+        total = lax.all_to_all(total.astype(jnp.bfloat16), "chip", 0, 0, tiled=False)
+        input_grad = jnp.sum(total.astype(jnp.float32), 0).astype(jnp.bfloat16)
         contract_first = (((0,), (0,)), ((), ()))
         gate_grad = lax.dot_general(
             all_inputs, gate_term, contract_first, preferred_element_type=jnp.float32

time: 256 us -> 237 us (0.926)
  waiting for transfers between devices: 92.8 us -> 74.5 us
    all_to_all x1, waiting for transfers between devices: 29.5 us -> 11.2 us  [per_device(): lax.all_to_all(total.astype(jnp.bfloat16), 'chip', 0, 0, tiled=False)]
  transfers between devices with their start and end apart: 2 -> 2, of which waited for: 2 -> 2; matrix products, arithmetic and copies ran while one was open for 4% -> 5% of each run, Pallas kernels for 0% -> 0%
where the time goes in v3:
time: 237 us
  blocking collectives  112 us (47%)
  waiting for transfers between devices  74.5 us (31%)
  matrix products  22.2 us (9%)
  between operations  14.2 us (6%)
  other arithmetic  6.76 us (3%)
  starting transfers between devices  5.32 us (2%)
    all_gather x1, waiting for transfers between devices, per_device(): lax.all_gather(jnp.concatenate([inputs, out_grad], 1), ('chip', 'core'),...  63.3 us
    all_to_all x1, blocking collectives, per_device(): lax.all_to_all(parts.reshape(n_wid, tokens // n_wid, 3 * ff), 'wid', 0, 0...  52.1 us
    all_to_all x1, blocking collectives, per_device(): lax.all_to_all(terms, 'wid', 0, 0, tiled=False).reshape(tokens, 3 * ff)  50.5 us
    all_to_all x1, waiting for transfers between devices, per_device(): lax.all_to_all(total.astype(jnp.bfloat16), 'chip', 0, 0, tiled=False)  11.2 us
    all_to_all x1, blocking collectives, per_device(): total = jnp.sum(lax.all_to_all(total, 'core', 1, 1, tiled=False), 1)  9.49 us
    all_to_all x1, starting transfers between devices, per_device(): lax.all_to_all(total.astype(jnp.bfloat16), 'chip', 0, 0, tiled=False)  5.28 us
    dot_general x1, matrix products, per_device(): lax.dot_general(all_inputs, gate_term, contract_first, preferred_element_...  5.03 us
  transfers between devices with their start and end apart: 2, of which 2 were waited for; matrix products, arithmetic and copies ran while one was open for 5% of the time, Pallas kernels for 0%

profile of v3, /device:TPU:1, one launch (start us, length us, event | category | flops | bytes accessed | tf_op | source)
XLA Modules:
  0.0 236.8 jit_solution(11559158547120793445)
XLA Ops:
  7.2 1.6 pad_maximum_fusion.2
  8.8 63.3 %all-gather.2.cloned.1.call-done = bf16[768,2048]{1,0:T(8,128)(2,1)} async-done(((bf16[24,2048]{1,0:T(8,128)(2,1)}), bf16[768,2048]{1,0:T(8,128)(2,1)}) %all-gather.2.cloned.1.call-update) | async-done | bytes 3145744 | tf_op jit(solution)/shard_map/all_gather | solution.py:19
  72.1 3.9 %convolution_convert_fusion.4 = bf16[768,896]{1,0:T(8,128)(2,1)S(1)} fusion(bf16[1024,896]{1,0:T(8,128)(2,1)} %param.7, bf16[768,2048]{1,0:T(8,128)(2,1)} %all-gather.2.cloned.1.call-done), kind=kOutput, calls=%fused_computation.7 | convolution fusion | flops 1409974272 | bytes 4784128 | tf_op jit(solution)/shard_map/dot_general | solution.py:24
  76.1 1.9 convolution_convert_fusion.3
  77.9 1.8 convolution_convert_fusion.5
  79.7 0.4 pad_maximum_fusion
  80.1 52.1 %all_to_all.20 = bf16[8,96,2688]{2,1,0:T(8,128)(2,1)S(1)} all-to-all(bf16[8,96,2688]{2,1,0:T(8,128)(2,1)S(1)} %pad_maximum_fusion), channel_id=1, replica_groups=mesh['chip'=16,'core'=2,'wid'=8] {'wid'}, dimensions={0} | all-to-all | bytes 8257536 | tf_op jit(solution)/shard_map/all_to_all | solution.py:29
  132.2 0.5 convert_reduce_fusion
  132.8 0.2 multiply_convert_fusion.2
  133.0 0.3 broadcast_in_dim.2
  133.3 50.5 %all_to_all.21 = bf16[8,96,2688]{2,1,0:T(8,128)(2,1)S(1)} all-to-all(bf16[8,96,2688]{2,1,0:T(8,128)(2,1)S(1)} %broadcast_in_dim.2), channel_id=1, replica_groups=mesh['chip'=16,'core'=2,'wid'=8] {'wid'}, dimensions={0} | all-to-all | bytes 8257536 | tf_op jit(solution)/shard_map/all_to_all | solution.py:34
  183.9 1.8 fusion.6
  185.7 0.2 copy-done.1
  185.9 0.8 copy-done.6
  186.7 1.8 convolution_add_fusion
  188.6 0.4 copy.10
  188.9 9.5 %all_to_all.22 = f32[16,2,24,1024]{3,2,0,1:T(8,128)} all-to-all(f32[16,2,24,1024]{3,2,0,1:T(8,128)S(1)} %copy.10), channel_id=1, replica_groups=mesh['chip'=16,'core'=2,'wid'=8] {'core'}, dimensions={1} | all-to-all | bytes 6291456 | tf_op jit(solution)/shard_map/all_to_all | solution.py:40
  198.4 3.3 %reduce_sum.31 = bf16[16,24,1024]{2,1,0:T(8,128)(2,1)} reduce(f32[16,2,24,1024]{3,2,0,1:T(8,128)} %all_to_all.22, f32[]{:T(128)} %constant.1.clone.1), dimensions={1}, to_apply=%region_1.0 | reduce | flops 393216 | bytes 3932164 | tf_op jit(solution)/shard_map/reduce_sum | solution.py:40
  201.7 5.3 %all-to-all-start.3 = ((bf16[16,24,1024]{2,1,0:T(8,128)(2,1)}), bf16[16,24,1024]{2,1,0:T(8,128)(2,1)S(1)}, u32[]{:S(2)}, u32[]{:S(2)}) async-start(bf16[16,24,1024]{2,1,0:T(8,128)(2,1)} %reduce_sum.31), calls=%async_computation.3 | async-start | bytes 1572864 | tf_op jit(solution)/shard_map/all_to_all | solution.py:41
  207.0 5.0 %convolution_convert_fusion.2 = bf16[1024,896]{1,0:T(8,128)(2,1)} fusion(bf16[768,2688]{1,0:T(8,128)(2,1)} %bitcast.12, bf16[768,2048]{1,0:T(8,128)(2,1)} %all-gather.2.cloned.1.call-done), kind=kOutput, calls=%fused_computation.4 | convolution fusion | flops 1410203648 | bytes 4784128 | tf_op jit(solution)/shard_map/dot_general | solution.py:44
  212.1 3.1 %convolution_convert_fusion.1 = bf16[1024,896]{1,0:T(8,128)(2,1)} fusion(bf16[768,2688]{1,0:T(8,128)(2,1)S(1)} %bitcast.13, bf16[768,2048]{1,0:T(8,128)(2,1)S(1)} %copy-done.4), kind=kOutput, calls=%fused_computation.3 | convolution fusion | flops 1410203648 | bytes 4784128 | tf_op jit(solution)/shard_map/dot_general | solution.py:47
  215.1 2.9 %convolution_convert_fusion = bf16[896,1024]{1,0:T(8,128)(2,1)} fusion(bf16[768,2048]{1,0:T(8,128)(2,1)S(1)} %copy-done.4, bf16[768,2688]{1,0:T(8,128)(2,1)S(1)} %bitcast.14), kind=kOutput, calls=%fused_computation.2 | convolution fusion | flops 1410203648 | bytes 4784128 | tf_op jit(solution)/shard_map/dot_general | solution.py:50
  218.0 11.2 %all-to-all-done.3 = bf16[16,24,1024]{2,1,0:T(8,128)(2,1)S(1)} async-done(((bf16[16,24,1024]{2,1,0:T(8,128)(2,1)}), bf16[16,24,1024]{2,1,0:T(8,128)(2,1)S(1)}, u32[]{:S(2)}, u32[]{:S(2)}) %all-to-all-start.3) | async-done | bytes 786464 | tf_op jit(solution)/shard_map/all_to_all | solution.py:41
  229.2 0.7 reduce_sum.32
  (15 shorter events, 0.1 us)
Async XLA Ops:
  7.2 70.8 %copy-start = (bf16[1024,896]{1,0:T(8,128)(2,1)S(1)}, bf16[1024,896]{1,0:T(8,128)(2,1)}, u32[]{:S(2)}) copy-start(bf16[1024,896]{1,0:T(8,128)(2,1)} %param.6) | copy-start | bytes 5505028
  7.2 64.9 %all-gather.2.cloned.1.call-start = ((), (), s32[]{:S(2)}) async-start(), calls=%async_computation.4 | async-start | bytes 3244032 | tf_op jit(solution)/shard_map/all_gather | solution.py:19
  72.1 3.9 %copy-start.3 = (bf16[768,2048]{1,0:T(8,128)(2,1)S(1)}, bf16[768,2048]{1,0:T(8,128)(2,1)}, u32[]{:S(2)}) copy-start(bf16[768,2048]{1,0:T(8,128)(2,1)} %all-gather.2.cloned.1.call-done) | copy-start | bytes 9437188
  72.1 3.9 %copy-start.5 = (bf16[896,1024]{1,0:T(8,128)(2,1)S(1)}, bf16[896,1024]{1,0:T(8,128)(2,1)}, u32[]{:S(2)}) copy-start(bf16[896,1024]{1,0:T(8,128)(2,1)} %param.8) | copy-start | bytes 5505028
  183.9 2.0 copy-start.1
  183.9 2.9 %copy-start.6 = (bf16[1024,896]{1,0:T(8,128)(2,1)S(1)}, bf16[1024,896]{1,0:T(8,128)(2,1)}, u32[]{:S(2)}) copy-start(bf16[1024,896]{1,0:T(8,128)(2,1)} %param.7) | copy-start | bytes 5505028
  201.7 27.5 %all-to-all-start.3 = ((bf16[16,24,1024]{2,1,0:T(8,128)(2,1)}), bf16[16,24,1024]{2,1,0:T(8,128)(2,1)S(1)}, u32[]{:S(2)}, u32[]{:S(2)}) async-start(bf16[16,24,1024]{2,1,0:T(8,128)(2,1)} %reduce_sum.31), calls=%async_computation.3 | async-start | bytes 1572864 | tf_op jit(solution)/shard_map/all_to_all | solution.py:41
  207.0 5.1 %copy-start.2 = (bf16[8,96,2688]{2,1,0:T(8,128)(2,1)S(1)}, bf16[8,96,2688]{2,1,0:T(8,128)(2,1)}, u32[]{:S(2)}) copy-start(bf16[8,96,2688]{2,1,0:T(8,128)(2,1)} %copy-done.1) | copy-start | bytes 12386308
  207.0 5.0 %copy-start.4 = (bf16[768,2048]{1,0:T(8,128)(2,1)S(1)}, bf16[768,2048]{1,0:T(8,128)(2,1)}, u32[]{:S(2)}) copy-start(bf16[768,2048]{1,0:T(8,128)(2,1)} %all-gather.2.cloned.1.call-done) | copy-start | bytes 9437188
Sparse Core Ops, SparseCore 0:
  11.1 60.9 all-gather.1

commit v4 on v3

v4 whole, which is shorter than its diff:
```python
import jax
import jax.numpy as jnp
from jax import lax
from jax.sharding import Mesh, PartitionSpec as P

HID = ("chip", "core")


def swiglu_terms(gate, up, hidden_grad):
    sigma = jax.nn.sigmoid(gate)
    hidden = (gate * sigma * up).astype(jnp.bfloat16)
    up_term = (hidden_grad * gate * sigma).astype(jnp.bfloat16)
    gate_term = (hidden_grad * up * sigma * (1.0 + gate * (1.0 - sigma))).astype(jnp.bfloat16)
    return (hidden, gate_term, up_term)


def make_per_device(n_hid, n_wid, n_chunk):
    def per_device(inputs, gate_weight, up_weight, down_weight, out_grad):
        rows, dw = inputs.shape
        ff = gate_weight.shape[1]
        rc = rows // n_chunk
        contract_last = (((1,), (1,)), ((), ()))
        both = jnp.concatenate([inputs, out_grad], 1)
        gathered, sums = [], []
        for k in range(n_chunk):
            g = lax.all_gather(both[k * rc:(k + 1) * rc], HID, axis=0, tiled=True)
            gathered.append(g)
            g_in, g_og = g[:, :dw], g[:, dw:]
            parts = jnp.concatenate([
                jnp.dot(g_in, gate_weight, preferred_element_type=jnp.float32),
                jnp.dot(g_in, up_weight, preferred_element_type=jnp.float32),
                lax.dot_general(g_og, down_weight, contract_last, preferred_element_type=jnp.float32),
            ], 1).astype(jnp.bfloat16)
            parts = lax.all_to_all(parts.reshape(n_wid, -1, 3 * ff), "wid", 0, 0, tiled=False)
            sums.append(jnp.sum(parts.astype(jnp.float32), 0))
        sums = jnp.stack(sums)
        gate, up, hidden_grad = sums[..., :ff], sums[..., ff:2 * ff], sums[..., 2 * ff:]
        terms = jnp.concatenate(swiglu_terms(gate, up, hidden_grad), -1)
        terms = jnp.broadcast_to(terms[None], (n_wid,) + terms.shape)
        terms = lax.all_to_all(terms, "wid", 0, 0, tiled=False)
        terms = jnp.swapaxes(terms, 0, 1).reshape(-1, 3 * ff)
        hidden, gate_term, up_term = terms[:, :ff], terms[:, ff:2 * ff], terms[:, 2 * ff:]
        gathered = jnp.concatenate(gathered, 0)
        all_inputs, all_grads = gathered[:, :dw], gathered[:, dw:]
        total = lax.dot_general(
            gate_term, gate_weight, contract_last, preferred_element_type=jnp.float32
        ) + lax.dot_general(up_term, up_weight, contract_last, preferred_element_type=jnp.float32)
        total = total.reshape(n_chunk, n_hid // 2, 2, rc, dw)
        total = jnp.sum(lax.all_to_all(total, "core", 2, 2, tiled=False), 2)
        total = lax.all_to_all(total.astype(jnp.bfloat16), "chip", 1, 1, tiled=False)
        input_grad = jnp.sum(total.astype(jnp.float32), 1).reshape(rows, dw).astype(jnp.bfloat16)
        contract_first = (((0,), (0,)), ((), ()))
        gate_grad = lax.dot_general(
            all_inputs, gate_term, contract_first, preferred_element_type=jnp.float32
        ).astype(jnp.bfloat16)
        up_grad = lax.dot_general(
            all_inputs, up_term, contract_first, preferred_element_type=jnp.float32
        ).astype(jnp.bfloat16)
        down_grad = lax.dot_general(
            hidden, all_grads, contract_first, preferred_element_type=jnp.float32
        ).astype(jnp.bfloat16)
        return (input_grad, gate_grad, up_grad, down_grad)

    return per_device


def solution(mesh):
    n_hid, n_wid = mesh.shape["hid"], mesh.shape["wid"]
    split = Mesh(mesh.devices.reshape(n_hid // 2, 2, n_wid), ("chip", "core", "wid"))
    placed = (P(HID, "wid"), P("wid", HID), P("wid", HID), P(HID, "wid"), P(HID, "wid"))
    return jax.shard_map(
        make_per_device(n_hid, n_wid, 2),
        mesh=split,
        in_specs=placed,
        out_specs=(P(HID, "wid"), P("wid", HID), P("wid", HID), P(HID, "wid")),
        check_vma=False,
    )
```

time: 237 us -> 290 us (1.22)
  the two profiles are of different devices: /device:TPU:1 before, /device:TPU:32 now
where the time goes in v4:
time: 290 us; the launch traced here: 289 us
  waiting for transfers between devices  177 us (61%)
  local copies, waits for them, and re-layouts  29.3 us (10%)
  matrix products  25.9 us (9%)
  starting transfers between devices  23.5 us (8%)
  between operations  14.2 us (5%)
  other arithmetic  12 us (4%)
  blocking collectives  7.24 us (2%)
    all_gather x2, waiting for transfers between devices, per_device(): g = lax.all_gather(both[k * rc:(k + 1) * rc], HID, axis=0, tiled=True)  96 us
    all_to_all x1, waiting for transfers between devices, per_device(): terms = lax.all_to_all(terms, 'wid', 0, 0, tiled=False)  44.8 us
    all_to_all x2, waiting for transfers between devices, per_device(): lax.all_to_all(parts.reshape(n_wid, -1, 3 * ff), 'wid', 0, 0, tiled=False)  23.2 us
    all_to_all x2, starting transfers between devices, per_device(): lax.all_to_all(parts.reshape(n_wid, -1, 3 * ff), 'wid', 0, 0, tiled=False)  13 us
    all_to_all x1, waiting for transfers between devices, per_device(): lax.all_to_all(total.astype(jnp.bfloat16), 'chip', 1, 1, tiled=False)  12.5 us
    unnamed x25, local copies, waits for them, and re-layouts  11.5 us
    reshape x2, local copies, waits for them, and re-layouts, per_device(): total = total.reshape(n_chunk, n_hid // 2, 2, rc, dw)  8.59 us
    all_to_all x1, blocking collectives, per_device(): total = jnp.sum(lax.all_to_all(total, 'core', 2, 2, tiled=False), 2)  7.24 us
  transfers between devices with their start and end apart: 6, of which 5 were waited for; matrix products, arithmetic and copies ran while one was open for 13% of the time, Pallas kernels for 0%

profile of v4, /device:TPU:32, one launch (start us, length us, event | category | flops | bytes accessed | tf_op | source)
XLA Modules:
  0.0 289.3 jit_solution(3518951935308546727)
XLA Ops:
  10.4 56.0 %all-gather.7.cloned.1.call-done = bf16[32,12,2048]{2,1,0:T(8,128)(2,1)} async-done(((bf16[1,12,2048]{2,1,0:T(8,128)(2,1)}), bf16[32,12,2048]{2,1,0:T(8,128)(2,1)}) %all-gather.7.cloned.1.call-update) | async-done | bytes 1572880 | tf_op jit(solution)/shard_map/all_gather | solution.py:26
  66.4 2.5 reshape.36
  68.9 2.6 convolution_convert_fusion.4
  75.0 6.9 %all-to-all-start.1 = ((bf16[8,48,2688]{2,1,0:T(8,128)(2,1)}), bf16[8,48,2688]{2,1,0:T(8,128)(2,1)}, u32[]{:S(2)}, u32[]{:S(2)}) async-start(bf16[8,48,2688]{2,1,0:T(8,128)(2,1)} %pad_maximum_fusion.1), calls=%async_computation.1 | async-start | bytes 4128768 | tf_op jit(solution)/shard_map/all_to_all | solution.py:34
  81.9 40.0 %all-gather.5.cloned.1.call-done = bf16[32,12,2048]{2,1,0:T(8,128)(2,1)} async-done(((bf16[1,12,2048]{2,1,0:T(8,128)(2,1)}), bf16[32,12,2048]{2,1,0:T(8,128)(2,1)}) %all-gather.5.cloned.1.call-update) | async-done | bytes 1572880 | tf_op jit(solution)/shard_map/all_gather | solution.py:26
  121.9 3.6 %reshape.34 = bf16[384,2048]{1,0:T(8,128)(2,1)} reshape(bf16[32,12,2048]{2,1,0:T(8,128)(2,1)} %all-gather.5.cloned.1.call-done) | data formatting | bytes 3145728
  125.6 2.9 convolution_convert_fusion.7
  131.9 6.2 %all-to-all-start = ((bf16[8,48,2688]{2,1,0:T(8,128)(2,1)}), bf16[8,48,2688]{2,1,0:T(8,128)(2,1)}, u32[]{:S(2)}, u32[]{:S(2)}) async-start(bf16[8,48,2688]{2,1,0:T(8,128)(2,1)} %pad_maximum_fusion), calls=%async_computation | async-start | bytes 4128768 | tf_op jit(solution)/shard_map/all_to_all | solution.py:34
  138.1 2.7 convert_reduce_fusion
  140.8 23.2 %all-to-all-done = bf16[8,48,2688]{2,1,0:T(8,128)(2,1)} async-done(((bf16[8,48,2688]{2,1,0:T(8,128)(2,1)}), bf16[8,48,2688]{2,1,0:T(8,128)(2,1)}, u32[]{:S(2)}, u32[]{:S(2)}) %all-to-all-start) | async-done | bytes 2064416 | tf_op jit(solution)/shard_map/all_to_all | solution.py:34
  168.5 5.0 %all-to-all-start.2 = ((bf16[8,2,48,2688]{3,2,1,0:T(8,128)(2,1)}), bf16[8,2,48,2688]{3,2,1,0:T(8,128)(2,1)}, u32[]{:S(2)}, u32[]{:S(2)}) async-start(bf16[8,2,48,2688]{3,2,1,0:T(8,128)(2,1)} %broadcast_in_dim.2), calls=%async_computation.2 | async-start | bytes 8257536 | tf_op jit(solution)/shard_map/all_to_all | solution.py:40
  173.5 2.8 constant_dynamic-update-slice_fusion.3
  176.2 44.8 %all-to-all-done.2 = bf16[8,2,48,2688]{3,2,1,0:T(8,128)(2,1)} async-done(((bf16[8,2,48,2688]{3,2,1,0:T(8,128)(2,1)}), bf16[8,2,48,2688]{3,2,1,0:T(8,128)(2,1)}, u32[]{:S(2)}, u32[]{:S(2)}) %all-to-all-start.2) | async-done | bytes 4128800 | tf_op jit(solution)/shard_map/all_to_all | solution.py:40
  221.0 2.5 copy.11
  226.4 3.6 %convolution_add_fusion = f32[768,1024]{1,0:T(8,128)} fusion(f32[768,1024]{1,0:T(8,128)S(1)} %fusion.7, bf16[1024,896]{1,0:T(8,128)(2,1)S(1)} %copy-done.9, bf16[768,2688]{1,0:T(8,128)(2,1)S(1)} %bitcast.24), kind=kOutput, calls=%fused_computation.7 | convolution fusion | flops 1410072576 | bytes 9502720 | tf_op jit(solution)/shard_map/dot_general | solution.py:47
  230.0 4.6 %reshape.32 = f32[2,16,2,12,1024]{4,3,2,1,0:T(8,128)} reshape(f32[768,1024]{1,0:T(8,128)} %convolution_add_fusion) | data formatting | bytes 6291456 | tf_op jit(solution)/shard_map/reshape | solution.py:48
  234.5 4.0 %copy.12 = f32[2,16,2,12,1024]{4,1,3,0,2:T(8,128)S(1)} copy(f32[2,16,2,12,1024]{4,3,2,1,0:T(8,128)} %reshape.32) | data formatting | bytes 6291456 | tf_op jit(solution)/shard_map/reshape | solution.py:48
  238.6 7.2 %all_to_all.25 = f32[2,16,2,12,1024]{4,1,3,0,2:T(8,128)} all-to-all(f32[2,16,2,12,1024]{4,1,3,0,2:T(8,128)S(1)} %copy.12), channel_id=1, replica_groups=mesh['chip'=16,'core'=2,'wid'=8] {'core'}, dimensions={2} | all-to-all | bytes 6291456 | tf_op jit(solution)/shard_map/all_to_all | solution.py:49
  245.8 2.3 reduce_sum.41
  249.8 5.4 %all-to-all-start.4 = ((bf16[2,16,12,1024]{3,0,2,1:T(2,128)(2,1)}), bf16[2,16,12,1024]{3,0,2,1:T(2,128)(2,1)}, u32[]{:S(2)}, u32[]{:S(2)}) async-start(bf16[2,16,12,1024]{3,0,2,1:T(2,128)(2,1)} %copy.13), calls=%async_computation.4 | async-start | bytes 1572864 | tf_op jit(solution)/shard_map/all_to_all | solution.py:50
  256.5 5.0 %convolution_convert_fusion.2 = bf16[1024,896]{1,0:T(8,128)(2,1)} fusion(bf16[768,2048]{1,0:T(8,128)(2,1)} %constant_dynamic-update-slice_fusion.2, bf16[768,2688]{1,0:T(8,128)(2,1)} %bitcast.25), kind=kOutput, calls=%fused_computation.6 | convolution fusion | flops 1410203648 | bytes 4784128 | tf_op jit(solution)/shard_map/dot_general | solution.py:53
  261.5 3.1 %convolution_convert_fusion.1 = bf16[1024,896]{1,0:T(8,128)(2,1)} fusion(bf16[768,2048]{1,0:T(8,128)(2,1)S(1)} %copy-done.6, bf16[768,2688]{1,0:T(8,128)(2,1)S(1)} %bitcast.26), kind=kOutput, calls=%fused_computation.5 | convolution fusion | flops 1410203648 | bytes 4784128 | tf_op jit(solution)/shard_map/dot_general | solution.py:56
  264.6 2.9 convolution_convert_fusion
  267.5 12.5 %all-to-all-done.4 = bf16[2,16,12,1024]{3,0,2,1:T(2,128)(2,1)} async-done(((bf16[2,16,12,1024]{3,0,2,1:T(2,128)(2,1)}), bf16[2,16,12,1024]{3,0,2,1:T(2,128)(2,1)}, u32[]{:S(2)}, u32[]{:S(2)}) %all-to-all-start.4) | async-done | bytes 786464 | tf_op jit(solution)/shard_map/all_to_all | solution.py:50
  (44 shorter events, 23.0 us)
Async XLA Ops:
  7.2 65.4 %copy-start = (bf16[1024,896]{1,0:T(8,128)(2,1)S(1)}, bf16[1024,896]{1,0:T(8,128)(2,1)}, u32[]{:S(2)}) copy-start(bf16[1024,896]{1,0:T(8,128)(2,1)} %param.6) | copy-start | bytes 5505028
  7.2 59.2 %all-gather.7.cloned.1.call-start = ((), (), s32[]{:S(2)}) async-start(), calls=%async_computation.6 | async-start | bytes 2162688 | tf_op jit(solution)/shard_map/all_gather | solution.py:26
  9.6 112.3 %all-gather.5.cloned.1.call-start = ((), (), s32[]{:S(2)}) async-start(), calls=%async_computation.5 | async-start | bytes 2162688 | tf_op jit(solution)/shard_map/all_gather | solution.py:26
  68.9 2.6 copy-start.7
  75.0 56.9 %all-to-all-start.1 = ((bf16[8,48,2688]{2,1,0:T(8,128)(2,1)}), bf16[8,48,2688]{2,1,0:T(8,128)(2,1)}, u32[]{:S(2)}, u32[]{:S(2)}) async-start(bf16[8,48,2688]{2,1,0:T(8,128)(2,1)} %pad_maximum_fusion.1), calls=%async_computation.1 | async-start | bytes 4128768 | tf_op jit(solution)/shard_map/all_to_all | solution.py:34
  125.6 2.9 copy-start.2
  125.6 2.9 copy-start.8
  131.9 32.1 %all-to-all-start = ((bf16[8,48,2688]{2,1,0:T(8,128)(2,1)}), bf16[8,48,2688]{2,1,0:T(8,128)(2,1)}, u32[]{:S(2)}, u32[]{:S(2)}) async-start(bf16[8,48,2688]{2,1,0:T(8,128)(2,1)} %pad_maximum_fusion), calls=%async_computation | async-start | bytes 4128768 | tf_op jit(solution)/shard_map/all_to_all | solution.py:34
  164.0 2.0 copy-start.5
  168.5 52.5 %all-to-all-start.2 = ((bf16[8,2,48,2688]{3,2,1,0:T(8,128)(2,1)}), bf16[8,2,48,2688]{3,2,1,0:T(8,128)(2,1)}, u32[]{:S(2)}, u32[]{:S(2)}) async-start(bf16[8,2,48,2688]{3,2,1,0:T(8,128)(2,1)} %broadcast_in_dim.2), calls=%async_computation.2 | async-start | bytes 8257536 | tf_op jit(solution)/shard_map/all_to_all | solution.py:40
  223.5 2.0 copy-start.3
  223.5 2.9 copy-start.9
  249.8 30.2 %all-to-all-start.4 = ((bf16[2,16,12,1024]{3,0,2,1:T(2,128)(2,1)}), bf16[2,16,12,1024]{3,0,2,1:T(2,128)(2,1)}, u32[]{:S(2)}, u32[]{:S(2)}) async-start(bf16[2,16,12,1024]{3,0,2,1:T(2,128)(2,1)} %copy.13), calls=%async_computation.4 | async-start | bytes 1572864 | tf_op jit(solution)/shard_map/all_to_all | solution.py:50
  256.5 5.0 %copy-start.4 = (bf16[8,2,48,2688]{3,2,0,1:T(8,128)(2,1)S(1)}, bf16[8,2,48,2688]{3,2,0,1:T(8,128)(2,1)}, u32[]{:S(2)}) copy-start(bf16[8,2,48,2688]{3,2,0,1:T(8,128)(2,1)} %copy-done.3) | copy-start | bytes 12386308
  256.5 5.0 %copy-start.6 = (bf16[768,2048]{1,0:T(8,128)(2,1)S(1)}, bf16[768,2048]{1,0:T(8,128)(2,1)}, u32[]{:S(2)}) copy-start(bf16[768,2048]{1,0:T(8,128)(2,1)} %constant_dynamic-update-slice_fusion.2) | copy-start | bytes 9437188
  264.6 17.9 %copy-start.1 = (bf16[1024,896]{1,0:T(8,128)(2,1)S(1)}, bf16[1024,896]{1,0:T(8,128)(2,1)}, u32[]{:S(2)}) copy-start(bf16[1024,896]{1,0:T(8,128)(2,1)} %param.6) | copy-start | bytes 5505028
Sparse Core Ops, SparseCore 0:
  11.1 55.2 all-gather.6
  69.5 52.4 all-gather.4

commit v5 on v3

--- a/solution.py
+++ b/solution.py
@@ -29,10 +29,12 @@
         parts = lax.all_to_all(parts.reshape(n_wid, tokens // n_wid, 3 * ff), "wid", 0, 0, tiled=False)
         sums = jnp.sum(parts.astype(jnp.float32), 0)
         gate, up, hidden_grad = sums[:, :ff], sums[:, ff:2 * ff], sums[:, 2 * ff:]
-        terms = jnp.concatenate(swiglu_terms(gate, up, hidden_grad), 1)
+        hidden, gate_term, up_term = swiglu_terms(gate, up, hidden_grad)
+        hidden = lax.all_gather(hidden, "wid", axis=0, tiled=True)
+        terms = jnp.concatenate([gate_term, up_term], 1)
         terms = jnp.broadcast_to(terms[None], (n_wid,) + terms.shape)
-        terms = lax.all_to_all(terms, "wid", 0, 0, tiled=False).reshape(tokens, 3 * ff)
-        hidden, gate_term, up_term = terms[:, :ff], terms[:, ff:2 * ff], terms[:, 2 * ff:]
+        terms = lax.all_to_all(terms, "wid", 0, 0, tiled=False).reshape(tokens, 2 * ff)
+        gate_term, up_term = terms[:, :ff], terms[:, ff:]
         total = lax.dot_general(
             gate_term, gate_weight, contract_last, preferred_element_type=jnp.float32
         ) + lax.dot_general(up_term, up_weight, contract_last, preferred_element_type=jnp.float32)

time: 237 us -> 235 us (level)
  the two profiles are of different devices: /device:TPU:1 before, /device:TPU:32 now
where the time goes in v5:
time: 235 us; the launch traced here: 234 us
  waiting for transfers between devices  110 us (47%)
  blocking collectives  61.4 us (26%)
  matrix products  27.7 us (12%)
  between operations  14.2 us (6%)
  starting transfers between devices  11.3 us (5%)
  other arithmetic  7.41 us (3%)
    all_gather x1, waiting for transfers between devices, per_device(): lax.all_gather(jnp.concatenate([inputs, out_grad], 1), ('chip', 'core'),...  60.5 us
    all_to_all x1, blocking collectives, per_device(): lax.all_to_all(parts.reshape(n_wid, tokens // n_wid, 3 * ff), 'wid', 0, 0...  54.2 us
    all_to_all x1, waiting for transfers between devices, per_device(): lax.all_to_all(terms, 'wid', 0, 0, tiled=False).reshape(tokens, 2 * ff)  37.8 us
    all_to_all x1, waiting for transfers between devices, per_device(): lax.all_to_all(total.astype(jnp.bfloat16), 'chip', 0, 0, tiled=False)  10.9 us
    all_to_all x1, blocking collectives, per_device(): total = jnp.sum(lax.all_to_all(total, 'core', 1, 1, tiled=False), 1)  7.22 us
    all_to_all x1, starting transfers between devices, per_device(): lax.all_to_all(terms, 'wid', 0, 0, tiled=False).reshape(tokens, 2 * ff)  5.74 us
    all_to_all x1, starting transfers between devices, per_device(): lax.all_to_all(total.astype(jnp.bfloat16), 'chip', 0, 0, tiled=False)  5.56 us
    dot_general x1, matrix products, per_device(): lax.dot_general(hidden, all_grads, contract_first, preferred_element_type...  4.83 us
  transfers between devices with their start and end apart: 4, of which 3 were waited for; matrix products, arithmetic and copies ran while one was open for 10% of the time, Pallas kernels for 0%

profile of v5, /device:TPU:32, one launch (start us, length us, event | category | flops | bytes accessed | tf_op | source)
XLA Modules:
  0.0 234.1 jit_solution(16126990112111897526)
XLA Ops:
  7.2 1.6 pad_maximum_fusion.2
  8.8 60.5 %all-gather.3.cloned.1.call-done = bf16[768,2048]{1,0:T(8,128)(2,1)} async-done(((bf16[24,2048]{1,0:T(8,128)(2,1)}), bf16[768,2048]{1,0:T(8,128)(2,1)}) %all-gather.3.cloned.1.call-update) | async-done | bytes 3145744 | tf_op jit(solution)/shard_map/all_gather | solution.py:19
  69.4 3.9 %convolution_convert_fusion.4 = bf16[768,896]{1,0:T(8,128)(2,1)S(1)} fusion(bf16[1024,896]{1,0:T(8,128)(2,1)} %param.7, bf16[768,2048]{1,0:T(8,128)(2,1)} %all-gather.3.cloned.1.call-done), kind=kOutput, calls=%fused_computation.7 | convolution fusion | flops 1409974272 | bytes 4784128 | tf_op jit(solution)/shard_map/dot_general | solution.py:24
  73.3 1.9 convolution_convert_fusion.3
  75.2 1.8 convolution_convert_fusion.5
  77.0 0.4 pad_maximum_fusion
  77.3 54.2 %all_to_all.20 = bf16[8,96,2688]{2,1,0:T(8,128)(2,1)S(1)} all-to-all(bf16[8,96,2688]{2,1,0:T(8,128)(2,1)S(1)} %pad_maximum_fusion), channel_id=1, replica_groups=mesh['chip'=16,'core'=2,'wid'=8] {'wid'}, dimensions={0} | all-to-all | bytes 8257536 | tf_op jit(solution)/shard_map/all_to_all | solution.py:29
  131.5 0.5 convert_reduce_fusion
  132.1 0.9 multiply_convert_fusion
  133.0 1.7 broadcast_in_dim.2
  134.7 5.7 %all-to-all-start.1 = ((bf16[8,96,1792]{2,1,0:T(8,128)(2,1)}), bf16[8,96,1792]{2,1,0:T(8,128)(2,1)}, u32[]{:S(2)}, u32[]{:S(2)}) async-start(bf16[8,96,1792]{2,1,0:T(8,128)(2,1)} %broadcast_in_dim.2), calls=%async_computation.1 | async-start | bytes 5505024 | tf_op jit(solution)/shard_map/all_to_all | solution.py:36
  140.4 0.7 all-gather.5.cloned.1.call-update
  141.2 37.8 %all-to-all-done.1 = bf16[8,96,1792]{2,1,0:T(8,128)(2,1)} async-done(((bf16[8,96,1792]{2,1,0:T(8,128)(2,1)}), bf16[8,96,1792]{2,1,0:T(8,128)(2,1)}, u32[]{:S(2)}, u32[]{:S(2)}) %all-to-all-start.1) | async-done | bytes 2752544 | tf_op jit(solution)/shard_map/all_to_all | solution.py:36
  178.9 3.3 %fusion.5 = f32[768,1024]{1,0:T(8,128)S(1)} fusion(bf16[1024,896]{1,0:T(8,128)(2,1)S(1)} %copy-done, bf16[768,1792]{1,0:T(8,128)(2,1)} %bitcast.3), kind=kOutput, calls=%fused_computation.14 | convolution fusion | flops 1409286144 | bytes 6356992 | tf_op jit(solution)/shard_map/dot_general | solution.py:38
  182.3 3.2 %convolution_add_fusion = f32[768,1024]{1,0:T(8,128)S(1)} fusion(f32[768,1024]{1,0:T(8,128)S(1)} %fusion.5, bf16[1024,896]{1,0:T(8,128)(2,1)S(1)} %copy-done.4, bf16[768,1792]{1,0:T(8,128)(2,1)} %bitcast.3), kind=kOutput, calls=%fused_computation.5 | convolution fusion | flops 1410072576 | bytes 9502720 | tf_op jit(solution)/shard_map/dot_general | solution.py:40
  185.5 0.4 copy.10
  185.9 7.2 %all_to_all.21 = f32[16,2,24,1024]{3,2,0,1:T(8,128)} all-to-all(f32[16,2,24,1024]{3,2,0,1:T(8,128)S(1)} %copy.10), channel_id=1, replica_groups=mesh['chip'=16,'core'=2,'wid'=8] {'core'}, dimensions={1} | all-to-all | bytes 6291456 | tf_op jit(solution)/shard_map/all_to_all | solution.py:42
  193.1 3.3 %reduce_sum.31 = bf16[16,24,1024]{2,1,0:T(8,128)(2,1)} reduce(f32[16,2,24,1024]{3,2,0,1:T(8,128)} %all_to_all.21, f32[]{:T(128)} %constant.1.clone.1), dimensions={1}, to_apply=%region_1.0 | reduce | flops 393216 | bytes 3932164 | tf_op jit(solution)/shard_map/reduce_sum | solution.py:42
  196.4 5.6 %all-to-all-start.3 = ((bf16[16,24,1024]{2,1,0:T(8,128)(2,1)}), bf16[16,24,1024]{2,1,0:T(8,128)(2,1)S(1)}, u32[]{:S(2)}, u32[]{:S(2)}) async-start(bf16[16,24,1024]{2,1,0:T(8,128)(2,1)} %reduce_sum.31), calls=%async_computation.3 | async-start | bytes 1572864 | tf_op jit(solution)/shard_map/all_to_all | solution.py:43
  202.0 4.8 %convolution_convert_fusion = bf16[896,1024]{1,0:T(8,128)(2,1)} fusion(bf16[768,896]{1,0:T(8,128)(2,1)} %all-gather.5.cloned.1.call-done, bf16[768,2048]{1,0:T(8,128)(2,1)} %all-gather.3.cloned.1.call-done), kind=kOutput, calls=%fused_computation.2 | convolution fusion | flops 1410203648 | bytes 4784128 | tf_op jit(solution)/shard_map/dot_general | solution.py:52
  206.8 4.4 %convolution_convert_fusion.2 = bf16[1024,896]{1,0:T(8,128)(2,1)} fusion(bf16[768,1792]{1,0:T(8,128)(2,1)} %bitcast.3, bf16[768,2048]{1,0:T(8,128)(2,1)S(1)} %copy-done.2), kind=kOutput, calls=%fused_computation.4 | convolution fusion | flops 1410203648 | bytes 4784128 | tf_op jit(solution)/shard_map/dot_general | solution.py:46
  211.2 4.4 %convolution_convert_fusion.1 = bf16[1024,896]{1,0:T(8,128)(2,1)} fusion(bf16[768,1792]{1,0:T(8,128)(2,1)} %bitcast.3, bf16[768,2048]{1,0:T(8,128)(2,1)S(1)} %copy-done.2), kind=kOutput, calls=%fused_computation.3 | convolution fusion | flops 1410203648 | bytes 4784128 | tf_op jit(solution)/shard_map/dot_general | solution.py:49
  215.7 10.9 %all-to-all-done.3 = bf16[16,24,1024]{2,1,0:T(8,128)(2,1)S(1)} async-done(((bf16[16,24,1024]{2,1,0:T(8,128)(2,1)}), bf16[16,24,1024]{2,1,0:T(8,128)(2,1)S(1)}, u32[]{:S(2)}, u32[]{:S(2)}) %all-to-all-start.3) | async-done | bytes 786464 | tf_op jit(solution)/shard_map/all_to_all | solution.py:43
  226.5 0.7 reduce_sum.32
  (15 shorter events, 0.1 us)
Async XLA Ops:
  7.2 68.0 %copy-start = (bf16[1024,896]{1,0:T(8,128)(2,1)S(1)}, bf16[1024,896]{1,0:T(8,128)(2,1)}, u32[]{:S(2)}) copy-start(bf16[1024,896]{1,0:T(8,128)(2,1)} %param.6) | copy-start | bytes 5505028
  7.2 62.2 %all-gather.3.cloned.1.call-start = ((), (), s32[]{:S(2)}) async-start(), calls=%async_computation.4 | async-start | bytes 3244032 | tf_op jit(solution)/shard_map/all_gather | solution.py:19
  69.3 3.9 %copy-start.1 = (bf16[768,2048]{1,0:T(8,128)(2,1)S(1)}, bf16[768,2048]{1,0:T(8,128)(2,1)}, u32[]{:S(2)}) copy-start(bf16[768,2048]{1,0:T(8,128)(2,1)} %all-gather.3.cloned.1.call-done) | copy-start | bytes 9437188
  69.3 3.9 %copy-start.3 = (bf16[896,1024]{1,0:T(8,128)(2,1)S(1)}, bf16[896,1024]{1,0:T(8,128)(2,1)}, u32[]{:S(2)}) copy-start(bf16[896,1024]{1,0:T(8,128)(2,1)} %param.8) | copy-start | bytes 5505028
  134.7 44.2 %all-to-all-start.1 = ((bf16[8,96,1792]{2,1,0:T(8,128)(2,1)}), bf16[8,96,1792]{2,1,0:T(8,128)(2,1)}, u32[]{:S(2)}, u32[]{:S(2)}) async-start(bf16[8,96,1792]{2,1,0:T(8,128)(2,1)} %broadcast_in_dim.2), calls=%async_computation.1 | async-start | bytes 5505024 | tf_op jit(solution)/shard_map/all_to_all | solution.py:36
  140.4 61.5 %all-gather.5.cloned.1.call-start = ((), (), s32[]{:S(2)}) async-start(), calls=%async_computation.5 | async-start | bytes 1548288 | tf_op jit(solution)/shard_map/all_gather | solution.py:33
  178.9 3.3 %copy-start.4 = (bf16[1024,896]{1,0:T(8,128)(2,1)S(1)}, bf16[1024,896]{1,0:T(8,128)(2,1)}, u32[]{:S(2)}) copy-start(bf16[1024,896]{1,0:T(8,128)(2,1)} %param.7) | copy-start | bytes 5505028
  196.4 30.2 %all-to-all-start.3 = ((bf16[16,24,1024]{2,1,0:T(8,128)(2,1)}), bf16[16,24,1024]{2,1,0:T(8,128)(2,1)S(1)}, u32[]{:S(2)}, u32[]{:S(2)}) async-start(bf16[16,24,1024]{2,1,0:T(8,128)(2,1)} %reduce_sum.31), calls=%async_computation.3 | async-start | bytes 1572864 | tf_op jit(solution)/shard_map/all_to_all | solution.py:43
  201.9 4.8 %copy-start.2 = (bf16[768,2048]{1,0:T(8,128)(2,1)S(1)}, bf16[768,2048]{1,0:T(8,128)(2,1)}, u32[]{:S(2)}) copy-start(bf16[768,2048]{1,0:T(8,128)(2,1)} %all-gather.3.cloned.1.call-done) | copy-start | bytes 9437188
Sparse Core Ops, SparseCore 0:
  11.1 58.1 all-gather.2
  143.6 48.2 all-gather.4

commit v6 on v5

--- a/solution.py
+++ b/solution.py
@@ -25,10 +25,13 @@
         grad_part = lax.dot_general(
             all_grads, down_weight, contract_last, preferred_element_type=jnp.float32
         )
-        parts = jnp.concatenate([gate_part, up_part, grad_part], 1).astype(jnp.bfloat16)
-        parts = lax.all_to_all(parts.reshape(n_wid, tokens // n_wid, 3 * ff), "wid", 0, 0, tiled=False)
+        hidden_grad = lax.psum_scatter(
+            grad_part.astype(jnp.bfloat16), "wid", scatter_dimension=0, tiled=True
+        ).astype(jnp.float32)
+        parts = jnp.concatenate([gate_part, up_part], 1).astype(jnp.bfloat16)
+        parts = lax.all_to_all(parts.reshape(n_wid, tokens // n_wid, 2 * ff), "wid", 0, 0, tiled=False)
         sums = jnp.sum(parts.astype(jnp.float32), 0)
-        gate, up, hidden_grad = sums[:, :ff], sums[:, ff:2 * ff], sums[:, 2 * ff:]
+        gate, up = sums[:, :ff], sums[:, ff:]
         hidden, gate_term, up_term = swiglu_terms(gate, up, hidden_grad)
         hidden = lax.all_gather(hidden, "wid", axis=0, tiled=True)
         terms = jnp.concatenate([gate_term, up_term], 1)

time: 235 us -> 239 us (1.017)
  blocking collectives: 61.4 us -> 7.24 us
  waiting for transfers between devices: 110 us -> 156 us
  starting transfers between devices: 11.3 us -> 17.4 us
  other arithmetic: 7.41 us -> 11.4 us
  matrix products: 27.7 us -> 30.7 us
    all_to_all x1 -> x0, blocking collectives: 54.2 us -> none  [per_device(): lax.all_to_all(parts.reshape(n_wid, tokens // n_wid, 3 * ff), 'wid', 0, 0...]
    all_to_all x0 -> x1, waiting for transfers between devices: none -> 34.1 us  [per_device(): lax.all_to_all(parts.reshape(n_wid, tokens // n_wid, 2 * ff), 'wid', 0, 0...]
    reduce_scatter x0 -> x1, waiting for transfers between devices: none -> 13.4 us  [per_device(): lax.psum_scatter(grad_part.astype(jnp.bfloat16), 'wid', scatter_dimension...]
    all_to_all x0 -> x1, starting transfers between devices: none -> 6.71 us  [per_device(): lax.all_to_all(parts.reshape(n_wid, tokens // n_wid, 2 * ff), 'wid', 0, 0...]
    dot_general x1, matrix products: 1.87 us -> 4.88 us  [per_device(): lax.dot_general(all_grads, down_weight, contract_last, preferred_element_...]
  transfers between devices with their start and end apart: 4 -> 6, of which waited for: 3 -> 5; matrix products, arithmetic and copies ran while one was open for 10% -> 13% of each run, Pallas kernels for 0% -> 0%
where the time goes in v6:
time: 239 us; the launch traced here: 238 us
  waiting for transfers between devices  156 us (65%)
  matrix products  30.7 us (13%)
  starting transfers between devices  17.4 us (7%)
  between operations  13.8 us (6%)
  other arithmetic  11.4 us (5%)
  blocking collectives  7.24 us (3%)
    all_gather x1, waiting for transfers between devices, per_device(): lax.all_gather(jnp.concatenate([inputs, out_grad], 1), ('chip', 'core'),...  60.5 us
    all_to_all x1, waiting for transfers between devices, per_device(): lax.all_to_all(terms, 'wid', 0, 0, tiled=False).reshape(tokens, 2 * ff)  36.1 us
    all_to_all x1, waiting for transfers between devices, per_device(): lax.all_to_all(parts.reshape(n_wid, tokens // n_wid, 2 * ff), 'wid', 0, 0...  34.1 us
    reduce_scatter x1, waiting for transfers between devices, per_device(): lax.psum_scatter(grad_part.astype(jnp.bfloat16), 'wid', scatter_dimension...  13.4 us
    all_to_all x1, waiting for transfers between devices, per_device(): lax.all_to_all(total.astype(jnp.bfloat16), 'chip', 0, 0, tiled=False)  10.8 us
    all_to_all x1, blocking collectives, per_device(): total = jnp.sum(lax.all_to_all(total, 'core', 1, 1, tiled=False), 1)  7.24 us
    all_to_all x1, starting transfers between devices, per_device(): lax.all_to_all(parts.reshape(n_wid, tokens // n_wid, 2 * ff), 'wid', 0, 0...  6.71 us
    all_to_all x1, starting transfers between devices, per_device(): lax.all_to_all(total.astype(jnp.bfloat16), 'chip', 0, 0, tiled=False)  5.61 us
  transfers between devices with their start and end apart: 6, of which 5 were waited for; matrix products, arithmetic and copies ran while one was open for 13% of the time, Pallas kernels for 0%

profile of v6, /device:TPU:32, one launch (start us, length us, event | category | flops | bytes accessed | tf_op | source)
XLA Modules:
  0.0 238.4 jit_solution(12148643991733243878)
XLA Ops:
  7.2 1.6 pad_maximum_fusion.2
  8.8 60.5 %all-gather.3.cloned.1.call-done = bf16[768,2048]{1,0:T(8,128)(2,1)} async-done(((bf16[24,2048]{1,0:T(8,128)(2,1)}), bf16[768,2048]{1,0:T(8,128)(2,1)}) %all-gather.3.cloned.1.call-update) | async-done | bytes 3145744 | tf_op jit(solution)/shard_map/all_gather | solution.py:19
  69.3 3.9 %convolution_convert_fusion.3 = bf16[768,896]{1,0:T(8,128)(2,1)S(1)} fusion(bf16[1024,896]{1,0:T(8,128)(2,1)} %param.7, bf16[768,2048]{1,0:T(8,128)(2,1)} %all-gather.3.cloned.1.call-done), kind=kOutput, calls=%fused_computation.6 | convolution fusion | flops 1409974272 | bytes 4784128 | tf_op jit(solution)/shard_map/dot_general | solution.py:24
  73.3 1.8 convolution_convert_fusion.4
  75.1 1.8 pad_maximum_fusion
  76.8 6.7 %all-to-all-start = ((bf16[8,96,1792]{2,1,0:T(8,128)(2,1)}), bf16[8,96,1792]{2,1,0:T(8,128)(2,1)}, u32[]{:S(2)}, u32[]{:S(2)}) async-start(bf16[8,96,1792]{2,1,0:T(8,128)(2,1)} %pad_maximum_fusion), calls=%async_computation.1 | async-start | bytes 5505024 | tf_op jit(solution)/shard_map/all_to_all | solution.py:32
  83.6 4.9 %convolution_convert_fusion.5 = bf16[768,896]{1,0:T(8,128)(2,1)} fusion(bf16[896,1024]{1,0:T(8,128)(2,1)} %param.8, bf16[768,2048]{1,0:T(8,128)(2,1)} %all-gather.3.cloned.1.call-done), kind=kOutput, calls=%fused_computation.8 | convolution fusion | flops 1409974272 | bytes 4784128 | tf_op jit(solution)/shard_map/dot_general | solution.py:25
  88.5 34.1 %all-to-all-done = bf16[8,96,1792]{2,1,0:T(8,128)(2,1)} async-done(((bf16[8,96,1792]{2,1,0:T(8,128)(2,1)}), bf16[8,96,1792]{2,1,0:T(8,128)(2,1)}, u32[]{:S(2)}, u32[]{:S(2)}) %all-to-all-start) | async-done | bytes 2752544 | tf_op jit(solution)/shard_map/all_to_all | solution.py:32
  122.6 2.2 convert_reduce_fusion
  124.8 13.4 %reduce-scatter.2.cloned.1.call-done = bf16[96,896]{1,0:T(8,128)(2,1)} async-done(((bf16[768,896]{1,0:T(8,128)(2,1)}), bf16[96,896]{1,0:T(8,128)(2,1)}) %reduce-scatter.2.cloned.1.call-update) | async-done | bytes 172048 | tf_op jit(solution)/shard_map/reduce_scatter | solution.py:28
  138.2 1.8 fusion.13
  140.0 1.8 broadcast_in_dim.2
  141.7 5.0 %all-to-all-start.1 = ((bf16[8,96,1792]{2,1,0:T(8,128)(2,1)}), bf16[8,96,1792]{2,1,0:T(8,128)(2,1)}, u32[]{:S(2)}, u32[]{:S(2)}) async-start(bf16[8,96,1792]{2,1,0:T(8,128)(2,1)} %broadcast_in_dim.2), calls=%async_computation.2 | async-start | bytes 5505024 | tf_op jit(solution)/shard_map/all_to_all | solution.py:39
  147.5 36.1 %all-to-all-done.1 = bf16[8,96,1792]{2,1,0:T(8,128)(2,1)} async-done(((bf16[8,96,1792]{2,1,0:T(8,128)(2,1)}), bf16[8,96,1792]{2,1,0:T(8,128)(2,1)}, u32[]{:S(2)}, u32[]{:S(2)}) %all-to-all-start.1) | async-done | bytes 2752544 | tf_op jit(solution)/shard_map/all_to_all | solution.py:39
  183.6 3.3 %fusion.5 = f32[768,1024]{1,0:T(8,128)S(1)} fusion(bf16[1024,896]{1,0:T(8,128)(2,1)S(1)} %copy-done, bf16[768,1792]{1,0:T(8,128)(2,1)} %bitcast.2), kind=kOutput, calls=%fused_computation.14 | convolution fusion | flops 1409286144 | bytes 6356992 | tf_op jit(solution)/shard_map/dot_general | solution.py:41
  186.9 3.2 %convolution_add_fusion = f32[768,1024]{1,0:T(8,128)S(1)} fusion(f32[768,1024]{1,0:T(8,128)S(1)} %fusion.5, bf16[1024,896]{1,0:T(8,128)(2,1)S(1)} %copy-done.3, bf16[768,1792]{1,0:T(8,128)(2,1)} %bitcast.2), kind=kOutput, calls=%fused_computation.5 | convolution fusion | flops 1410072576 | bytes 9502720 | tf_op jit(solution)/shard_map/dot_general | solution.py:43
  190.5 7.2 %all_to_all.20 = f32[16,2,24,1024]{3,2,0,1:T(8,128)} all-to-all(f32[16,2,24,1024]{3,2,0,1:T(8,128)S(1)} %copy.10), channel_id=1, replica_groups=mesh['chip'=16,'core'=2,'wid'=8] {'core'}, dimensions={1} | all-to-all | bytes 6291456 | tf_op jit(solution)/shard_map/all_to_all | solution.py:45
  197.7 3.3 %reduce_sum.31 = bf16[16,24,1024]{2,1,0:T(8,128)(2,1)} reduce(f32[16,2,24,1024]{3,2,0,1:T(8,128)} %all_to_all.20, f32[]{:T(128)} %constant.1.clone.1), dimensions={1}, to_apply=%region_2.0 | reduce | flops 393216 | bytes 3932164 | tf_op jit(solution)/shard_map/reduce_sum | solution.py:45
  201.0 5.6 %all-to-all-start.3 = ((bf16[16,24,1024]{2,1,0:T(8,128)(2,1)}), bf16[16,24,1024]{2,1,0:T(8,128)(2,1)S(1)}, u32[]{:S(2)}, u32[]{:S(2)}) async-start(bf16[16,24,1024]{2,1,0:T(8,128)(2,1)} %reduce_sum.31), calls=%async_computation.4 | async-start | bytes 1572864 | tf_op jit(solution)/shard_map/all_to_all | solution.py:46
  206.6 4.8 %convolution_convert_fusion = bf16[896,1024]{1,0:T(8,128)(2,1)} fusion(bf16[768,896]{1,0:T(8,128)(2,1)} %all-gather.5.cloned.1.call-done, bf16[768,2048]{1,0:T(8,128)(2,1)} %all-gather.3.cloned.1.call-done), kind=kOutput, calls=%fused_computation.2 | convolution fusion | flops 1410203648 | bytes 4784128 | tf_op jit(solution)/shard_map/dot_general | solution.py:55
  211.5 4.4 %convolution_convert_fusion.2 = bf16[1024,896]{1,0:T(8,128)(2,1)} fusion(bf16[768,1792]{1,0:T(8,128)(2,1)} %bitcast.2, bf16[768,2048]{1,0:T(8,128)(2,1)S(1)} %copy-done.2), kind=kOutput, calls=%fused_computation.4 | convolution fusion | flops 1410203648 | bytes 4784128 | tf_op jit(solution)/shard_map/dot_general | solution.py:49
  215.9 4.4 %convolution_convert_fusion.1 = bf16[1024,896]{1,0:T(8,128)(2,1)} fusion(bf16[768,1792]{1,0:T(8,128)(2,1)} %bitcast.2, bf16[768,2048]{1,0:T(8,128)(2,1)S(1)} %copy-done.2), kind=kOutput, calls=%fused_computation.3 | convolution fusion | flops 1410203648 | bytes 4784128 | tf_op jit(solution)/shard_map/dot_general | solution.py:52
  220.3 10.8 %all-to-all-done.3 = bf16[16,24,1024]{2,1,0:T(8,128)(2,1)S(1)} async-done(((bf16[16,24,1024]{2,1,0:T(8,128)(2,1)}), bf16[16,24,1024]{2,1,0:T(8,128)(2,1)S(1)}, u32[]{:S(2)}, u32[]{:S(2)}) %all-to-all-start.3) | async-done | bytes 786464 | tf_op jit(solution)/shard_map/all_to_all | solution.py:46
  231.1 0.7 reduce_sum.32
  (17 shorter events, 1.2 us)
Async XLA Ops:
  7.2 66.1 %copy-start = (bf16[1024,896]{1,0:T(8,128)(2,1)S(1)}, bf16[1024,896]{1,0:T(8,128)(2,1)}, u32[]{:S(2)}) copy-start(bf16[1024,896]{1,0:T(8,128)(2,1)} %param.6) | copy-start | bytes 5505028
  7.2 62.2 %all-gather.3.cloned.1.call-start = ((), (), s32[]{:S(2)}) async-start(), calls=%async_computation.5 | async-start | bytes 3244032 | tf_op jit(solution)/shard_map/all_gather | solution.py:19
  69.3 3.9 %copy-start.1 = (bf16[768,2048]{1,0:T(8,128)(2,1)S(1)}, bf16[768,2048]{1,0:T(8,128)(2,1)}, u32[]{:S(2)}) copy-start(bf16[768,2048]{1,0:T(8,128)(2,1)} %all-gather.3.cloned.1.call-done) | copy-start | bytes 9437188
  76.8 45.7 %all-to-all-start = ((bf16[8,96,1792]{2,1,0:T(8,128)(2,1)}), bf16[8,96,1792]{2,1,0:T(8,128)(2,1)}, u32[]{:S(2)}, u32[]{:S(2)}) async-start(bf16[8,96,1792]{2,1,0:T(8,128)(2,1)} %pad_maximum_fusion), calls=%async_computation.1 | async-start | bytes 5505024 | tf_op jit(solution)/shard_map/all_to_all | solution.py:32
  83.6 54.6 %reduce-scatter.2.cloned.1.call-start = ((), (), s32[]{:S(2)}) async-start(), calls=%async_computation.6 | async-start | bytes 1548288 | tf_op jit(solution)/shard_map/reduce_scatter | solution.py:28
  141.7 41.8 %all-to-all-start.1 = ((bf16[8,96,1792]{2,1,0:T(8,128)(2,1)}), bf16[8,96,1792]{2,1,0:T(8,128)(2,1)}, u32[]{:S(2)}, u32[]{:S(2)}) async-start(bf16[8,96,1792]{2,1,0:T(8,128)(2,1)} %broadcast_in_dim.2), calls=%async_computation.2 | async-start | bytes 5505024 | tf_op jit(solution)/shard_map/all_to_all | solution.py:39
  146.7 59.9 %all-gather.5.cloned.1.call-start = ((), (), s32[]{:S(2)}) async-start(), calls=%async_computation.7 | async-start | bytes 1548288 | tf_op jit(solution)/shard_map/all_gather | solution.py:36
  183.6 3.3 %copy-start.3 = (bf16[1024,896]{1,0:T(8,128)(2,1)S(1)}, bf16[1024,896]{1,0:T(8,128)(2,1)}, u32[]{:S(2)}) copy-start(bf16[1024,896]{1,0:T(8,128)(2,1)} %param.7) | copy-start | bytes 5505028
  201.0 30.1 %all-to-all-start.3 = ((bf16[16,24,1024]{2,1,0:T(8,128)(2,1)}), bf16[16,24,1024]{2,1,0:T(8,128)(2,1)S(1)}, u32[]{:S(2)}, u32[]{:S(2)}) async-start(bf16[16,24,1024]{2,1,0:T(8,128)(2,1)} %reduce_sum.31), calls=%async_computation.4 | async-start | bytes 1572864 | tf_op jit(solution)/shard_map/all_to_all | solution.py:46
  206.6 4.8 %copy-start.2 = (bf16[768,2048]{1,0:T(8,128)(2,1)S(1)}, bf16[768,2048]{1,0:T(8,128)(2,1)}, u32[]{:S(2)}) copy-start(bf16[768,2048]{1,0:T(8,128)(2,1)} %all-gather.3.cloned.1.call-done) | copy-start | bytes 9437188
Sparse Core Ops, SparseCore 0:
  11.1 58.1 all-gather.2
  88.6 49.5 reduce-scatter.1
  149.9 46.4 all-gather.4

commit v7 on v5

--- a/solution.py
+++ b/solution.py
@@ -39,7 +39,8 @@
             gate_term, gate_weight, contract_last, preferred_element_type=jnp.float32
         ) + lax.dot_general(up_term, up_weight, contract_last, preferred_element_type=jnp.float32)
         total = total.reshape(n_hid // 2, 2, tokens // n_hid, dw)
-        total = jnp.sum(lax.all_to_all(total, "core", 1, 1, tiled=False), 1)
+        total = lax.all_to_all(total.astype(jnp.bfloat16), "core", 1, 1, tiled=False)
+        total = jnp.sum(total.astype(jnp.float32), 1)
         total = lax.all_to_all(total.astype(jnp.bfloat16), "chip", 0, 0, tiled=False)
         input_grad = jnp.sum(total.astype(jnp.float32), 0).astype(jnp.bfloat16)
         contract_first = (((0,), (0,)), ((), ()))

time: 235 us -> 230 us (0.979)
  transfers between devices with their start and end apart: 4 -> 4, of which waited for: 3 -> 3; matrix products, arithmetic and copies ran while one was open for 10% -> 9% of each run, Pallas kernels for 0% -> 0%
where the time goes in v7:
time: 230 us; the launch traced here: 229 us
  waiting for transfers between devices  110 us (48%)
  blocking collectives  59.2 us (26%)
  matrix products  27.2 us (12%)
  between operations  14.2 us (6%)
  starting transfers between devices  11.3 us (5%)
  other arithmetic  5.57 us (2%)
    all_gather x1, waiting for transfers between devices, per_device(): lax.all_gather(jnp.concatenate([inputs, out_grad], 1), ('chip', 'core'),...  60.5 us
    all_to_all x1, blocking collectives, per_device(): lax.all_to_all(parts.reshape(n_wid, tokens // n_wid, 3 * ff), 'wid', 0, 0...  54.2 us
    all_to_all x1, waiting for transfers between devices, per_device(): lax.all_to_all(terms, 'wid', 0, 0, tiled=False).reshape(tokens, 2 * ff)  37.8 us
    all_to_all x1, waiting for transfers between devices, per_device(): lax.all_to_all(total.astype(jnp.bfloat16), 'chip', 0, 0, tiled=False)  10.9 us
    all_to_all x1, starting transfers between devices, per_device(): lax.all_to_all(terms, 'wid', 0, 0, tiled=False).reshape(tokens, 2 * ff)  5.73 us
    all_to_all x1, starting transfers between devices, per_device(): lax.all_to_all(total.astype(jnp.bfloat16), 'chip', 0, 0, tiled=False)  5.55 us
    all_to_all x1, blocking collectives, per_device(): lax.all_to_all(total.astype(jnp.bfloat16), 'core', 1, 1, tiled=False)  5 us
    dot_general x1, matrix products, per_device(): lax.dot_general(hidden, all_grads, contract_first, preferred_element_type...  4.83 us
  transfers between devices with their start and end apart: 4, of which 3 were waited for; matrix products, arithmetic and copies ran while one was open for 9% of the time, Pallas kernels for 0%

profile of v7, /device:TPU:32, one launch (start us, length us, event | category | flops | bytes accessed | tf_op | source)
XLA Modules:
  0.0 229.2 jit_solution(1545510910116339636)
XLA Ops:
  7.2 1.6 pad_maximum_fusion.2
  8.8 60.5 %all-gather.3.cloned.1.call-done = bf16[768,2048]{1,0:T(8,128)(2,1)} async-done(((bf16[24,2048]{1,0:T(8,128)(2,1)}), bf16[768,2048]{1,0:T(8,128)(2,1)}) %all-gather.3.cloned.1.call-update) | async-done | bytes 3145744 | tf_op jit(solution)/shard_map/all_gather | solution.py:19
  69.4 3.3 %convolution_convert_fusion.5 = bf16[768,896]{1,0:T(8,128)(2,1)S(1)} fusion(bf16[1024,896]{1,0:T(8,128)(2,1)S(1)} %copy-done, bf16[768,2048]{1,0:T(8,128)(2,1)} %all-gather.3.cloned.1.call-done), kind=kOutput, calls=%fused_computation.8 | convolution fusion | flops 1409974272 | bytes 4784128 | tf_op jit(solution)/shard_map/dot_general | solution.py:23
  72.7 1.8 convolution_convert_fusion.4
  74.5 1.9 convolution_convert_fusion.3
  76.4 0.4 pad_maximum_fusion
  76.8 54.2 %all_to_all.20 = bf16[8,96,2688]{2,1,0:T(8,128)(2,1)S(1)} all-to-all(bf16[8,96,2688]{2,1,0:T(8,128)(2,1)S(1)} %pad_maximum_fusion), channel_id=1, replica_groups=mesh['chip'=16,'core'=2,'wid'=8] {'wid'}, dimensions={0} | all-to-all | bytes 8257536 | tf_op jit(solution)/shard_map/all_to_all | solution.py:29
  131.0 0.5 convert_reduce_fusion
  131.5 0.9 multiply_convert_fusion
  132.4 1.8 broadcast_in_dim.2
  134.2 5.7 %all-to-all-start.1 = ((bf16[8,96,1792]{2,1,0:T(8,128)(2,1)}), bf16[8,96,1792]{2,1,0:T(8,128)(2,1)}, u32[]{:S(2)}, u32[]{:S(2)}) async-start(bf16[8,96,1792]{2,1,0:T(8,128)(2,1)} %broadcast_in_dim.2), calls=%async_computation.1 | async-start | bytes 5505024 | tf_op jit(solution)/shard_map/all_to_all | solution.py:36
  139.9 0.7 all-gather.5.cloned.1.call-update
  140.6 37.8 %all-to-all-done.1 = bf16[8,96,1792]{2,1,0:T(8,128)(2,1)} async-done(((bf16[8,96,1792]{2,1,0:T(8,128)(2,1)}), bf16[8,96,1792]{2,1,0:T(8,128)(2,1)}, u32[]{:S(2)}, u32[]{:S(2)}) %all-to-all-start.1) | async-done | bytes 2752544 | tf_op jit(solution)/shard_map/all_to_all | solution.py:36
  178.4 3.3 %fusion.5 = f32[768,1024]{1,0:T(8,128)S(1)} fusion(bf16[1024,896]{1,0:T(8,128)(2,1)S(1)} %copy-done, bf16[768,1792]{1,0:T(8,128)(2,1)} %bitcast.3), kind=kOutput, calls=%fused_computation.14 | convolution fusion | flops 1409286144 | bytes 6356992 | tf_op jit(solution)/shard_map/dot_general | solution.py:38
  181.7 3.2 %add_convert_fusion = bf16[768,1024]{1,0:T(8,128)(2,1)S(1)} fusion(f32[768,1024]{1,0:T(8,128)S(1)} %fusion.5, bf16[1024,896]{1,0:T(8,128)(2,1)S(1)} %copy-done.5, bf16[768,1792]{1,0:T(8,128)(2,1)} %bitcast.3), kind=kOutput, calls=%fused_computation.2 | convolution fusion | flops 1410859008 | bytes 7929856 | tf_op jit(solution)/shard_map/dot_general | solution.py:40
  184.9 0.1 copy.10
  185.1 5.0 %all_to_all.21 = bf16[16,2,24,1024]{3,2,0,1:T(8,128)(2,1)S(1)} all-to-all(bf16[16,2,24,1024]{3,2,0,1:T(8,128)(2,1)S(1)} %copy.10), channel_id=1, replica_groups=mesh['chip'=16,'core'=2,'wid'=8] {'core'}, dimensions={1} | all-to-all | bytes 3145728 | tf_op jit(solution)/shard_map/all_to_all | solution.py:42
  190.1 1.4 reduce_sum.34
  191.5 5.6 %all-to-all-start.3 = ((bf16[16,24,1024]{2,1,0:T(8,128)(2,1)}), bf16[16,24,1024]{2,1,0:T(8,128)(2,1)S(1)}, u32[]{:S(2)}, u32[]{:S(2)}) async-start(bf16[16,24,1024]{2,1,0:T(8,128)(2,1)} %reduce_sum.34), calls=%async_computation.3 | async-start | bytes 1572864 | tf_op jit(solution)/shard_map/all_to_all | solution.py:44
  197.1 4.8 %convolution_convert_fusion = bf16[896,1024]{1,0:T(8,128)(2,1)} fusion(bf16[768,896]{1,0:T(8,128)(2,1)} %all-gather.5.cloned.1.call-done, bf16[768,2048]{1,0:T(8,128)(2,1)} %all-gather.3.cloned.1.call-done), kind=kOutput, calls=%fused_computation.3 | convolution fusion | flops 1410203648 | bytes 4784128 | tf_op jit(solution)/shard_map/dot_general | solution.py:53
  201.9 4.4 %convolution_convert_fusion.1 = bf16[1024,896]{1,0:T(8,128)(2,1)} fusion(bf16[768,1792]{1,0:T(8,128)(2,1)} %bitcast.3, bf16[768,2048]{1,0:T(8,128)(2,1)S(1)} %copy-done.2), kind=kOutput, calls=%fused_computation.4 | convolution fusion | flops 1410203648 | bytes 4784128 | tf_op jit(solution)/shard_map/dot_general | solution.py:50
  206.4 4.4 %convolution_convert_fusion.2 = bf16[1024,896]{1,0:T(8,128)(2,1)} fusion(bf16[768,1792]{1,0:T(8,128)(2,1)} %bitcast.3, bf16[768,2048]{1,0:T(8,128)(2,1)S(1)} %copy-done.2), kind=kOutput, calls=%fused_computation.5 | convolution fusion | flops 1410203648 | bytes 4784128 | tf_op jit(solution)/shard_map/dot_general | solution.py:47
  210.8 10.9 %all-to-all-done.3 = bf16[16,24,1024]{2,1,0:T(8,128)(2,1)S(1)} async-done(((bf16[16,24,1024]{2,1,0:T(8,128)(2,1)}), bf16[16,24,1024]{2,1,0:T(8,128)(2,1)S(1)}, u32[]{:S(2)}, u32[]{:S(2)}) %all-to-all-start.3) | async-done | bytes 786464 | tf_op jit(solution)/shard_map/all_to_all | solution.py:44
  221.6 0.7 reduce_sum.35
  (17 shorter events, 0.1 us)
Async XLA Ops:
  7.2 62.2 %copy-start = (bf16[1024,896]{1,0:T(8,128)(2,1)S(1)}, bf16[1024,896]{1,0:T(8,128)(2,1)}, u32[]{:S(2)}) copy-start(bf16[1024,896]{1,0:T(8,128)(2,1)} %param.6) | copy-start | bytes 5505028
  7.2 62.2 %all-gather.3.cloned.1.call-start = ((), (), s32[]{:S(2)}) async-start(), calls=%async_computation.4 | async-start | bytes 3244032 | tf_op jit(solution)/shard_map/all_gather | solution.py:19
  69.3 3.4 %copy-start.1 = (bf16[768,2048]{1,0:T(8,128)(2,1)S(1)}, bf16[768,2048]{1,0:T(8,128)(2,1)}, u32[]{:S(2)}) copy-start(bf16[768,2048]{1,0:T(8,128)(2,1)} %all-gather.3.cloned.1.call-done) | copy-start | bytes 9437188
  69.4 3.4 %copy-start.4 = (bf16[1024,896]{1,0:T(8,128)(2,1)S(1)}, bf16[1024,896]{1,0:T(8,128)(2,1)}, u32[]{:S(2)}) copy-start(bf16[1024,896]{1,0:T(8,128)(2,1)} %param.7) | copy-start | bytes 5505028
  72.7 1.8 copy-start.3
  134.2 44.2 %all-to-all-start.1 = ((bf16[8,96,1792]{2,1,0:T(8,128)(2,1)}), bf16[8,96,1792]{2,1,0:T(8,128)(2,1)}, u32[]{:S(2)}, u32[]{:S(2)}) async-start(bf16[8,96,1792]{2,1,0:T(8,128)(2,1)} %broadcast_in_dim.2), calls=%async_computation.1 | async-start | bytes 5505024 | tf_op jit(solution)/shard_map/all_to_all | solution.py:36
  139.9 57.2 %all-gather.5.cloned.1.call-start = ((), (), s32[]{:S(2)}) async-start(), calls=%async_computation.5 | async-start | bytes 1548288 | tf_op jit(solution)/shard_map/all_gather | solution.py:33
  178.4 3.3 %copy-start.5 = (bf16[1024,896]{1,0:T(8,128)(2,1)S(1)}, bf16[1024,896]{1,0:T(8,128)(2,1)}, u32[]{:S(2)}) copy-start(bf16[1024,896]{1,0:T(8,128)(2,1)} %param.7) | copy-start | bytes 5505028
  191.5 30.2 %all-to-all-start.3 = ((bf16[16,24,1024]{2,1,0:T(8,128)(2,1)}), bf16[16,24,1024]{2,1,0:T(8,128)(2,1)S(1)}, u32[]{:S(2)}, u32[]{:S(2)}) async-start(bf16[16,24,1024]{2,1,0:T(8,128)(2,1)} %reduce_sum.34), calls=%async_computation.3 | async-start | bytes 1572864 | tf_op jit(solution)/shard_map/all_to_all | solution.py:44
  197.1 4.8 %copy-start.2 = (bf16[768,2048]{1,0:T(8,128)(2,1)S(1)}, bf16[768,2048]{1,0:T(8,128)(2,1)}, u32[]{:S(2)}) copy-start(bf16[768,2048]{1,0:T(8,128)(2,1)} %all-gather.3.cloned.1.call-done) | copy-start | bytes 9437188
Sparse Core Ops, SparseCore 0:
  11.1 58.1 all-gather.2
  143.1 48.2 all-gather.4

commit v8 on v5

--- a/solution.py
+++ b/solution.py
@@ -35,11 +35,19 @@
         terms = jnp.broadcast_to(terms[None], (n_wid,) + terms.shape)
         terms = lax.all_to_all(terms, "wid", 0, 0, tiled=False).reshape(tokens, 2 * ff)
         gate_term, up_term = terms[:, :ff], terms[:, ff:]
-        total = lax.dot_general(
-            gate_term, gate_weight, contract_last, preferred_element_type=jnp.float32
-        ) + lax.dot_general(up_term, up_weight, contract_last, preferred_element_type=jnp.float32)
-        total = total.reshape(n_hid // 2, 2, tokens // n_hid, dw)
-        total = jnp.sum(lax.all_to_all(total, "core", 1, 1, tiled=False), 1)
+        core = lax.axis_index("core")
+        by_core = (n_hid // 2, 2, tokens // n_hid, ff)
+
+        def rows_of(which):
+            g = lax.dynamic_index_in_dim(gate_term.reshape(by_core), which, 1, keepdims=False)
+            u = lax.dynamic_index_in_dim(up_term.reshape(by_core), which, 1, keepdims=False)
+            return lax.dot_general(
+                g.reshape(-1, ff), gate_weight, contract_last, preferred_element_type=jnp.float32
+            ) + lax.dot_general(u.reshape(-1, ff), up_weight, contract_last, preferred_element_type=jnp.float32)
+
+        sent = lax.ppermute(rows_of(1 - core).astype(jnp.bfloat16), "core", [(0, 1), (1, 0)])
+        total = rows_of(core) + sent.astype(jnp.float32)
+        total = total.reshape(n_hid // 2, tokens // n_hid, dw)
         total = lax.all_to_all(total.astype(jnp.bfloat16), "chip", 0, 0, tiled=False)
         input_grad = jnp.sum(total.astype(jnp.float32), 0).astype(jnp.bfloat16)
         contract_first = (((0,), (0,)), ((), ()))

time: 235 us -> 226 us (0.962)
  blocking collectives: 61.4 us -> 54.2 us
  other arithmetic: 7.41 us -> 4.13 us
  local copies, waits for them, and re-layouts: 2.15 us -> 4.54 us
    all_to_all x1 -> x0, blocking collectives: 7.22 us -> none  [per_device(): total = jnp.sum(lax.all_to_all(total, 'core', 1, 1, tiled=False), 1)]
    reduce_sum x1 -> x0, other arithmetic: 3.27 us -> none  [per_device(): total = jnp.sum(lax.all_to_all(total, 'core', 1, 1, tiled=False), 1)]
    dot_general x2 -> x4, matrix products: 6.49 us -> 4.94 us  [the longest x2 2.91 us: rows_of(): lax.dot_general(u.reshape(-1, ff), up_weight, contract_last, preferred_el...]
  transfers between devices with their start and end apart: 4 -> 5, of which waited for: 3 -> 4; matrix products, arithmetic and copies ran while one was open for 10% -> 9% of each run, Pallas kernels for 0% -> 0%
where the time goes in v8:
time: 226 us
  waiting for transfers between devices  111 us (49%)
  blocking collectives  54.2 us (24%)
  matrix products  26.2 us (12%)
  between operations  14.2 us (6%)
  starting transfers between devices  11.4 us (5%)
  local copies, waits for them, and re-layouts  4.54 us (2%)
  other arithmetic  4.13 us (2%)
    all_gather x1, waiting for transfers between devices, per_device(): lax.all_gather(jnp.concatenate([inputs, out_grad], 1), ('chip', 'core'),...  60.5 us
    all_to_all x1, blocking collectives, per_device(): lax.all_to_all(parts.reshape(n_wid, tokens // n_wid, 3 * ff), 'wid', 0, 0...  54.2 us
    all_to_all x1, waiting for transfers between devices, per_device(): lax.all_to_all(terms, 'wid', 0, 0, tiled=False).reshape(tokens, 2 * ff)  37.8 us
    all_to_all x1, waiting for transfers between devices, per_device(): lax.all_to_all(total.astype(jnp.bfloat16), 'chip', 0, 0, tiled=False)  10.9 us
    all_to_all x1, starting transfers between devices, per_device(): lax.all_to_all(terms, 'wid', 0, 0, tiled=False).reshape(tokens, 2 * ff)  5.75 us
    all_to_all x1, starting transfers between devices, per_device(): lax.all_to_all(total.astype(jnp.bfloat16), 'chip', 0, 0, tiled=False)  5.56 us
    dot_general x1, matrix products, per_device(): lax.dot_general(hidden, all_grads, contract_first, preferred_element_type...  4.83 us
  transfers between devices with their start and end apart: 5, of which 4 were waited for; matrix products, arithmetic and copies ran while one was open for 9% of the time, Pallas kernels for 0%

profile of v8, /device:TPU:32, one launch (start us, length us, event | category | flops | bytes accessed | tf_op | source)
XLA Modules:
  0.0 225.8 jit_solution(1284275522411784669)
XLA Ops:
  7.2 1.6 pad_maximum_fusion.2
  8.8 60.5 %all-gather.3.cloned.1.call-done = bf16[768,2048]{1,0:T(8,128)(2,1)} async-done(((bf16[24,2048]{1,0:T(8,128)(2,1)}), bf16[768,2048]{1,0:T(8,128)(2,1)}) %all-gather.3.cloned.1.call-update) | async-done | bytes 3145744 | tf_op jit(solution)/shard_map/all_gather | solution.py:19
  69.4 3.9 %convolution_convert_fusion.4 = bf16[768,896]{1,0:T(8,128)(2,1)S(1)} fusion(bf16[1024,896]{1,0:T(8,128)(2,1)} %param.7, bf16[768,2048]{1,0:T(8,128)(2,1)} %all-gather.3.cloned.1.call-done), kind=kOutput, calls=%fused_computation.6 | convolution fusion | flops 1409974272 | bytes 4784128 | tf_op jit(solution)/shard_map/dot_general | solution.py:24
  73.3 1.9 convolution_convert_fusion.3
  75.2 1.8 convolution_convert_fusion.5
  77.3 54.2 %all_to_all.15 = bf16[8,96,2688]{2,1,0:T(8,128)(2,1)S(1)} all-to-all(bf16[8,96,2688]{2,1,0:T(8,128)(2,1)S(1)} %pad_maximum_fusion), channel_id=1, replica_groups=mesh['chip'=16,'core'=2,'wid'=8] {'wid'}, dimensions={0} | all-to-all | bytes 8257536 | tf_op jit(solution)/shard_map/all_to_all | solution.py:29
  131.5 0.5 convert_reduce_fusion
  132.1 0.9 multiply_convert_fusion
  133.0 1.8 broadcast_in_dim.2
  134.7 5.7 %all-to-all-start.1 = ((bf16[8,96,1792]{2,1,0:T(8,128)(2,1)}), bf16[8,96,1792]{2,1,0:T(8,128)(2,1)}, u32[]{:S(2)}, u32[]{:S(2)}) async-start(bf16[8,96,1792]{2,1,0:T(8,128)(2,1)} %broadcast_in_dim.2), calls=%async_computation.1 | async-start | bytes 5505024 | tf_op jit(solution)/shard_map/all_to_all | solution.py:36
  140.5 0.7 all-gather.5.cloned.1.call-update
  141.2 37.8 %all-to-all-done.1 = bf16[8,96,1792]{2,1,0:T(8,128)(2,1)} async-done(((bf16[8,96,1792]{2,1,0:T(8,128)(2,1)}), bf16[8,96,1792]{2,1,0:T(8,128)(2,1)}, u32[]{:S(2)}, u32[]{:S(2)}) %all-to-all-start.1) | async-done | bytes 2752544 | tf_op jit(solution)/shard_map/all_to_all | solution.py:36
  179.0 2.0 fusion.8
  181.3 1.0 fusion.10
  182.8 1.0 add_convert_fusion.1
  183.9 1.0 fusion.9
  184.9 1.2 collective-permute-done
  186.2 1.9 add_convert_fusion
  188.1 5.6 %all-to-all-start.2 = ((bf16[16,24,1024]{2,1,0:T(8,128)(2,1)}), bf16[16,24,1024]{2,1,0:T(8,128)(2,1)S(1)}, u32[]{:S(2)}, u32[]{:S(2)}) async-start(bf16[16,24,1024]{2,1,0:T(8,128)(2,1)} %bitcast.10), calls=%async_computation.2 | async-start | bytes 1572864 | tf_op jit(solution)/shard_map/all_to_all | solution.py:51
  193.7 4.8 %convolution_convert_fusion = bf16[896,1024]{1,0:T(8,128)(2,1)} fusion(bf16[768,896]{1,0:T(8,128)(2,1)} %all-gather.5.cloned.1.call-done, bf16[768,2048]{1,0:T(8,128)(2,1)} %all-gather.3.cloned.1.call-done), kind=kOutput, calls=%fused_computation.2 | convolution fusion | flops 1410203648 | bytes 4784128 | tf_op jit(solution)/shard_map/dot_general | solution.py:60
  198.5 4.4 %convolution_convert_fusion.1 = bf16[1024,896]{1,0:T(8,128)(2,1)} fusion(bf16[768,2048]{1,0:T(8,128)(2,1)S(1)} %copy-done.2, bf16[768,1792]{1,0:T(8,128)(2,1)} %bitcast.3), kind=kOutput, calls=%fused_computation.3 | convolution fusion | flops 1410203648 | bytes 4784128 | tf_op jit(solution)/shard_map/dot_general | solution.py:57
  202.9 4.4 %convolution_convert_fusion.2 = bf16[1024,896]{1,0:T(8,128)(2,1)} fusion(bf16[768,2048]{1,0:T(8,128)(2,1)S(1)} %copy-done.2, bf16[768,1792]{1,0:T(8,128)(2,1)} %bitcast.3), kind=kOutput, calls=%fused_computation.4 | convolution fusion | flops 1410203648 | bytes 4784128 | tf_op jit(solution)/shard_map/dot_general | solution.py:54
  207.4 10.9 %all-to-all-done.2 = bf16[16,24,1024]{2,1,0:T(8,128)(2,1)S(1)} async-done(((bf16[16,24,1024]{2,1,0:T(8,128)(2,1)}), bf16[16,24,1024]{2,1,0:T(8,128)(2,1)S(1)}, u32[]{:S(2)}, u32[]{:S(2)}) %all-to-all-start.2) | async-done | bytes 786464 | tf_op jit(solution)/shard_map/all_to_all | solution.py:51
  218.2 0.7 reduce_sum.22
  (18 shorter events, 1.3 us)
Async XLA Ops:
  7.2 68.0 %copy-start = (bf16[1024,896]{1,0:T(8,128)(2,1)S(1)}, bf16[1024,896]{1,0:T(8,128)(2,1)}, u32[]{:S(2)}) copy-start(bf16[1024,896]{1,0:T(8,128)(2,1)} %param.6) | copy-start | bytes 5505028
  7.2 62.2 %all-gather.3.cloned.1.call-start = ((), (), s32[]{:S(2)}) async-start(), calls=%async_computation.3 | async-start | bytes 3244032 | tf_op jit(solution)/shard_map/all_gather | solution.py:19
  69.3 3.9 %copy-start.1 = (bf16[768,2048]{1,0:T(8,128)(2,1)S(1)}, bf16[768,2048]{1,0:T(8,128)(2,1)}, u32[]{:S(2)}) copy-start(bf16[768,2048]{1,0:T(8,128)(2,1)} %all-gather.3.cloned.1.call-done) | copy-start | bytes 9437188
  69.3 3.9 %copy-start.3 = (bf16[896,1024]{1,0:T(8,128)(2,1)S(1)}, bf16[896,1024]{1,0:T(8,128)(2,1)}, u32[]{:S(2)}) copy-start(bf16[896,1024]{1,0:T(8,128)(2,1)} %param.8) | copy-start | bytes 5505028
  134.7 44.3 %all-to-all-start.1 = ((bf16[8,96,1792]{2,1,0:T(8,128)(2,1)}), bf16[8,96,1792]{2,1,0:T(8,128)(2,1)}, u32[]{:S(2)}, u32[]{:S(2)}) async-start(bf16[8,96,1792]{2,1,0:T(8,128)(2,1)} %broadcast_in_dim.2), calls=%async_computation.1 | async-start | bytes 5505024 | tf_op jit(solution)/shard_map/all_to_all | solution.py:36
  140.5 53.2 %all-gather.5.cloned.1.call-start = ((), (), s32[]{:S(2)}) async-start(), calls=%async_computation.4 | async-start | bytes 1548288 | tf_op jit(solution)/shard_map/all_gather | solution.py:33
  181.3 1.5 copy-start.4
  183.8 2.4 %collective-permute-start = (bf16[384,1024]{1,0:T(8,128)(2,1)S(1)}, bf16[384,1024]{1,0:T(8,128)(2,1)S(1)}, u32[]{:S(2)}, u32[]{:S(2)}) collective-permute-start(bf16[384,1024]{1,0:T(8,128)(2,1)S(1)} %add_convert_fusion.1), channel_id=1, source_target_pairs={{0,8},{8,0},{1,9},{9,1},{2,10},{10,2},{3,11},{11,3},{4,12},{12,4},... | collective-permute-start | bytes 2359304 | tf_op jit(solution)/shard_map/ppermute | solution.py:48
  188.1 30.2 %all-to-all-start.2 = ((bf16[16,24,1024]{2,1,0:T(8,128)(2,1)}), bf16[16,24,1024]{2,1,0:T(8,128)(2,1)S(1)}, u32[]{:S(2)}, u32[]{:S(2)}) async-start(bf16[16,24,1024]{2,1,0:T(8,128)(2,1)} %bitcast.10), calls=%async_computation.2 | async-start | bytes 1572864 | tf_op jit(solution)/shard_map/all_to_all | solution.py:51
  193.7 4.8 %copy-start.2 = (bf16[768,2048]{1,0:T(8,128)(2,1)S(1)}, bf16[768,2048]{1,0:T(8,128)(2,1)}, u32[]{:S(2)}) copy-start(bf16[768,2048]{1,0:T(8,128)(2,1)} %all-gather.3.cloned.1.call-done) | copy-start | bytes 9437188
Sparse Core Ops, SparseCore 0:
  11.1 58.1 all-gather.2
  143.7 48.2 all-gather.4
